TPU v7x, 1024 devices: a whole 4x4x32 slice. The times are simulated.
1024 devices in a mesh: ta: 64 (over z, core), gz: 16 (over y, x).
Axes of the slice: x: 4, y: 4, z: 32, core: 2. Of those that a mesh axis runs over, the one named last changes fastest.
Arguments:
- source: bfloat16 [2, 4, 3, 64, 64, 512], P(None, None, None, 'ta', 'gz'), may hold values from -6 to 6
- gauge_links: bfloat16 [4, 2, 3, 3, 64, 64, 512], P(None, None, None, None, 'ta', 'gz'), may hold values from -2.5 to 2.5
- clover_diag: float32 [4, 3, 64, 64, 512], P(None, None, 'ta', 'gz'), may hold values from 0.5 to 4
- agg_map: int32 [64, 64, 512], P('ta', 'gz'), may hold values from 0 to 31
- prolong: bfloat16 [24, 2, 4, 3, 64, 64, 512], P(None, None, None, None, 'ta', 'gz'), may hold values from -0.0390625 to 0.0390625
- coarse_inverse: float32 [64, 768, 768], P('ta', 'gz'), may hold values from -24 to 24
Outputs:
- solution: float32 [2, 4, 3, 64, 64, 512], P(None, None, None, 'ta', 'gz')
Inputs may be any that keep to these rules, and one draw needn't show every extreme that they name: `agg_map`: aggregate numbers are local to each group of 16 devices along gz.
All inputs are finite; a program needn't handle non-finite values.
Results may differ from a plain program's by a relative error of at most 0.03.
Values may be sent and summed in bfloat16 or wider, within the bound.
No kernel may reach another device: no remote copies, remote signals or barrier semaphores. Data moves between devices by JAX's collectives and lax.ppermute only.
A program may use at most 32 MiB of HBM per device.

v0:
```python
import jax
import jax.numpy as jnp
from jax import lax
from jax.sharding import PartitionSpec as P

LX = 32
LY = 16
NAGG = 32


mass_shift = -0.4
spin_perms = ((3, 2, 1, 0), (3, 2, 1, 0), (2, 3, 0, 1), (2, 3, 0, 1))
spin_real = (
    (0.0, 0.0, 0.0, 0.0),
    (-1.0, 1.0, 1.0, -1.0),
    (0.0, 0.0, 0.0, 0.0),
    (1.0, 1.0, 1.0, 1.0),
)
spin_imag = (
    (-1.0, -1.0, 1.0, 1.0),
    (0.0, 0.0, 0.0, 0.0),
    (-1.0, 1.0, 1.0, -1.0),
    (0.0, 0.0, 0.0, 0.0),
)


def shifted(block, axis, distance):
    devices = range(lax.axis_size(axis))
    route = [((i - distance) % len(devices), i) for i in devices]
    return lax.ppermute(block, axis, route)


def phase_mul(coef_re, coef_im, value_re, value_im):
    if coef_im == 0.0:
        return (coef_re * value_re, coef_re * value_im)
    return (-coef_im * value_im, coef_im * value_re)


def project(wide, direction, sign):
    rows_re = []
    rows_im = []
    for slot in range(2):
        other = spin_perms[direction][slot]
        term_re, term_im = phase_mul(
            spin_real[direction][slot], spin_imag[direction][slot], wide[0, other], wide[1, other]
        )
        rows_re.append(wide[0, slot] + sign * term_re)
        rows_im.append(wide[1, slot] + sign * term_im)
    return jnp.stack([jnp.stack(rows_re), jnp.stack(rows_im)])


def expand(half, direction, sign):
    rows_re = [None] * 4
    rows_im = [None] * 4
    for slot in range(2):
        other = spin_perms[direction][slot]
        rows_re[slot] = half[0, slot]
        rows_im[slot] = half[1, slot]
        term_re, term_im = phase_mul(
            spin_real[direction][other], spin_imag[direction][other], half[0, slot], half[1, slot]
        )
        rows_re[other] = sign * term_re
        rows_im[other] = sign * term_im
    return jnp.stack([jnp.stack(rows_re), jnp.stack(rows_im)])


def color_mix(link_pair, spinor, dagger):
    link_re = link_pair[0].astype(jnp.float32)
    link_im = link_pair[1].astype(jnp.float32)
    spin_re = spinor[0].astype(jnp.float32)
    spin_im = spinor[1].astype(jnp.float32)
    out_re = []
    out_im = []
    for row in range(3):
        acc_re = None
        acc_im = None
        for col in range(3):
            if dagger:
                entry_re = link_re[col, row]
                entry_im = -link_im[col, row]
            else:
                entry_re = link_re[row, col]
                entry_im = link_im[row, col]
            part_re = entry_re * spin_re[:, col] - entry_im * spin_im[:, col]
            part_im = entry_re * spin_im[:, col] + entry_im * spin_re[:, col]
            acc_re = part_re if acc_re is None else acc_re + part_re
            acc_im = part_im if acc_im is None else acc_im + part_im
        out_re.append(acc_re)
        out_im.append(acc_im)
    return jnp.stack([jnp.stack(out_re, axis=1), jnp.stack(out_im, axis=1)])


def local_shift(values, direction, step):
    dims_all = values.shape
    grid = values.reshape(dims_all[:-1] + (LY, LX))
    rolled = jnp.roll(grid, -step, axis=-1 if direction == 0 else -2)
    return rolled.reshape(dims_all)


def fwd_round(wide, direction):
    return lax.optimization_barrier(project(wide, direction, -1.0).astype(jnp.bfloat16))


def hopping(spinor, gauge_links):
    wide = spinor.astype(jnp.float32)
    total = jnp.zeros(spinor.shape, jnp.float32)
    back_space = lax.optimization_barrier(
        project(color_mix(gauge_links[2], spinor, True), 2, 1.0).astype(jnp.bfloat16)
    )
    back_time = lax.optimization_barrier(
        project(color_mix(gauge_links[3], spinor, True), 3, 1.0).astype(jnp.bfloat16)
    )
    send_bz = expand(back_space.astype(jnp.float32), 2, 1.0).astype(jnp.bfloat16)
    send_bt = expand(back_time.astype(jnp.float32), 3, 1.0).astype(jnp.bfloat16)
    ahead_time = shifted(spinor, "ta", -1)
    fwd_time = jnp.concatenate([spinor[:, :, :, 1:], ahead_time], axis=3)
    behind_time = shifted(send_bt, "ta", 1)
    bwd_time = jnp.concatenate([behind_time, send_bt[:, :, :, :-1]], axis=3)
    ahead_space = shifted(spinor[:, :, :, :, 0:1], "gz", -1)
    fwd_space = jnp.concatenate([spinor[:, :, :, :, 1:], ahead_space], axis=4)
    behind_space = shifted(send_bz[:, :, :, :, -1:], "gz", 1)
    bwd_space = jnp.concatenate([behind_space, send_bz[:, :, :, :, :-1]], axis=4)
    fwd_space = fwd_round(fwd_space.astype(jnp.float32), 2)
    fwd_time = fwd_round(fwd_time.astype(jnp.float32), 3)
    bwd_space = bwd_space[:, 0:2]
    bwd_time = bwd_time[:, 0:2]
    for direction in range(2):
        ahead = local_shift(fwd_round(wide, direction), direction, 1)
        total = total + expand(color_mix(gauge_links[direction], ahead, False), direction, -1.0)
        back_half = lax.optimization_barrier(
            project(color_mix(gauge_links[direction], spinor, True), direction, 1.0).astype(
                jnp.bfloat16
            )
        )
        behind = local_shift(back_half, direction, -1).astype(jnp.float32)
        total = total + expand(behind, direction, 1.0)
    total = total + expand(color_mix(gauge_links[2], fwd_space, False), 2, -1.0)
    total = total + expand(bwd_space.astype(jnp.float32), 2, 1.0)
    total = total + expand(color_mix(gauge_links[3], fwd_time, False), 3, -1.0)
    total = total + expand(bwd_time.astype(jnp.float32), 3, 1.0)
    return total


def shards(source, gauge_links, clover_diag, agg_map, prolong, coarse_inverse):
    highest = lax.Precision.HIGHEST
    diagonal = 4.0 + mass_shift + clover_diag
    source_wide = source.astype(jnp.float32)
    first_iter = source_wide / diagonal
    first_half = first_iter.astype(jnp.bfloat16)
    first_resid = source_wide - diagonal * first_iter + 0.5 * hopping(first_half, gauge_links)
    second_iter = first_iter + first_resid / diagonal
    second_half = second_iter.astype(jnp.bfloat16)
    second_resid = source_wide - diagonal * second_iter + 0.5 * hopping(second_half, gauge_links)
    resid_half = second_resid.astype(jnp.bfloat16)
    projected = jnp.einsum(
        "vrsctzn,rsctzn->vtzn", prolong, resid_half, preferred_element_type=jnp.float32
    )
    vectors = prolong.shape[0]
    labels = jnp.arange(NAGG, dtype=jnp.int32)
    member = agg_map.reshape(-1)[None, :] == labels[:, None]
    partial_sum = jnp.einsum(
        "am,vm->av", member.astype(jnp.float32), projected.reshape(vectors, -1), precision=highest
    )
    coarse_resid = lax.psum(partial_sum.reshape(-1), "gz")
    own_rows = jnp.dot(coarse_inverse[0], coarse_resid, precision=highest)
    correction = lax.all_gather(own_rows, "gz", axis=0, tiled=True)
    correction_half = correction.astype(jnp.bfloat16).reshape(NAGG, vectors)
    spread = jnp.einsum(
        "av,am->vm",
        correction_half,
        member.astype(jnp.bfloat16),
        preferred_element_type=jnp.float32,
    ).astype(jnp.bfloat16)
    smooth = jnp.einsum(
        "vrsctzn,vtzn->rsctzn",
        prolong,
        spread.reshape(projected.shape),
        preferred_element_type=jnp.float32,
    )
    return second_iter + smooth


def solution(mesh):
    return jax.shard_map(
        shards,
        mesh=mesh,
        in_specs=(
            P(None, None, None, "ta", "gz", None),
            P(None, None, None, None, "ta", "gz", None),
            P(None, None, "ta", "gz", None),
            P("ta", "gz", None),
            P(None, None, None, None, "ta", "gz", None),
            P("ta", "gz", None),
        ),
        out_specs=P(None, None, None, "ta", "gz", None),
        check_vma=False,
    )
```

profile of v0, /device:TPU:2, one launch (start us, length us, event | category | flops | bytes accessed | tf_op | source)
XLA Modules:
  0.0 152.4 jit_solution(1619214731811988949)
XLA Ops:
  0.0 1.0 add_bitcast_fusion
  1.0 1.0 fusion.280
  1.9 16.2 %collective-permute-start.2 = (bf16[2,4,3,1,4,512]{5,4,2,3,1,0:T(4,128)(2,1)S(1)}, bf16[2,4,3,1,4,512]{5,4,2,3,1,0:T(4,128)(2,1)S(1)}, u32[]{:S(2)}, u32[]{:S(2)}) collective-permute-start(bf16[2,4,3,1,4,512]{5,4,2,3,1,0:T(4,128)(2,1)S(1)} %get-tuple-element.9), channel_id=1, source_target_pairs={{16,0},{32,16},{48,32},{64,48},{80,64},{96,80},{112,96},{128,112},... | collective-permute-start | bytes 294920 | tf_op jit(solution)/shard_map/ppermute | solution.py:30
  18.1 0.6 slice.2542
  18.8 2.4 %collective-permute-start = (bf16[2,4,3,1,1,512]{5,4,2,3,1,0:T(2,128)(2,1)}, bf16[2,4,3,1,1,512]{5,4,2,3,1,0:T(2,128)(2,1)}, u32[]{:S(2)}, u32[]{:S(2)}) collective-permute-start(bf16[2,4,3,1,1,512]{5,4,2,3,1,0:T(2,128)(2,1)} %slice.2542), channel_id=1, source_target_pairs={{1,0},{2,1},{3,2},{4,3},{5,4},{6,5},{7,6},{8,7},{9,8},{10,9},{11,1... | collective-permute-start | bytes 73736 | tf_op jit(solution)/shard_map/ppermute | solution.py:30
  21.3 0.9 bitcast_convert_fusion.9
  22.9 0.7 fusion.38
  23.6 3.4 %collective-permute-start.1 = (bf16[2,4,3,1,1,512]{5,4,2,3,1,0:T(2,128)(2,1)}, bf16[2,4,3,1,1,512]{5,4,2,3,1,0:T(2,128)(2,1)}, u32[]{:S(2)}, u32[]{:S(2)}) collective-permute-start(bf16[2,4,3,1,1,512]{5,4,2,3,1,0:T(2,128)(2,1)} %fusion.38), channel_id=1, source_target_pairs={{15,0},{0,1},{1,2},{2,3},{3,4},{4,5},{5,6},{6,7},{7,8},{8,9},{9,10... | collective-permute-start | bytes 73736 | tf_op jit(solution)/shard_map/ppermute | solution.py:30
  27.8 0.2 reshape.7015
  27.9 0.1 slice.1197
  28.1 0.1 fusion.31
  28.2 0.1 reshape.7030
  28.3 0.1 reshape.7032
  29.1 0.2 reshape.7016
  29.3 0.1 slice.1244
  29.4 0.1 maximum_convert_fusion
  29.6 0.2 reshape.7035
  29.9 0.2 reshape.7017
  30.3 0.1 reshape.7037
  30.4 0.1 reshape.7039
  31.2 0.2 reshape.7018
  31.4 0.1 maximum_convert_fusion.1
  31.5 0.2 reshape.7040
  32.1 1.3 copy.342
  33.4 1.3 dynamic-slice
  35.4 0.9 maximum_convert_fusion.4
  36.7 0.8 fusion.42
  38.2 0.8 slice_convert_fusion.1
  39.1 0.3 bitcast_convert_fusion.10
  39.6 0.2 reshape.7019
  39.8 0.1 slice.2661
  39.9 0.1 fusion.27
  40.1 0.1 reshape.7061
  40.2 0.1 reshape.7062
  41.0 0.2 reshape.7020
  41.1 0.1 slice.2691
  41.2 0.1 maximum_convert_fusion.2
  41.4 0.2 reshape.7065
  41.7 0.2 reshape.7021
  42.1 0.1 reshape.7066
  42.2 0.1 reshape.7067
  43.0 0.2 reshape.7022
  43.2 0.1 maximum_convert_fusion.3
  43.3 0.2 reshape.7068
  44.0 2.9 %collective-permute-start.6 = (bf16[2,4,3,1,4,512]{5,4,3,2,1,0:T(4,128)(2,1)S(1)}, bf16[2,4,3,1,4,512]{5,4,3,2,1,0:T(4,128)(2,1)S(1)}, u32[]{:S(2)}, u32[]{:S(2)}) collective-permute-start(bf16[2,4,3,1,4,512]{5,4,3,2,1,0:T(4,128)(2,1)S(1)} %get-tuple-element.6), channel_id=1, source_target_pairs={{16,0},{32,16},{48,32},{64,48},{80,64},{96,80},{112,96},{128,112},... | collective-permute-start | bytes 294920 | tf_op jit(solution)/shard_map/ppermute | solution.py:30
  47.3 5.6 %collective-permute-start.4 = (bf16[2,4,3,1,1,512]{5,4,2,3,1,0:T(2,128)(2,1)S(1)}, bf16[2,4,3,1,1,512]{5,4,2,3,1,0:T(2,128)(2,1)S(1)}, u32[]{:S(2)}, u32[]{:S(2)}) collective-permute-start(bf16[2,4,3,1,1,512]{5,4,2,3,1,0:T(2,128)(2,1)S(1)} %slice.2726), channel_id=1, source_target_pairs={{1,0},{2,1},{3,2},{4,3},{5,4},{6,5},{7,6},{8,7},{9,8},{10,9},{11,1... | collective-permute-start | bytes 73736 | tf_op jit(solution)/shard_map/ppermute | solution.py:30
  53.0 0.1 fusion.37
  53.1 2.1 %collective-permute-start.5 = (bf16[2,4,3,1,1,512]{5,4,2,1,3,0:T(2,128)(2,1)S(1)}, bf16[2,4,3,1,1,512]{5,4,2,1,3,0:T(2,128)(2,1)S(1)}, u32[]{:S(2)}, u32[]{:S(2)}) collective-permute-start(bf16[2,4,3,1,1,512]{5,4,2,1,3,0:T(2,128)(2,1)S(1)} %fusion.37), channel_id=1, source_target_pairs={{15,0},{0,1},{1,2},{2,3},{3,4},{4,5},{5,6},{6,7},{7,8},{8,9},{9,10... | collective-permute-start | bytes 73736 | tf_op jit(solution)/shard_map/ppermute | solution.py:30
  55.9 0.1 maximum_convert_fusion.5
  56.4 5.9 %collective-permute-done.5 = bf16[2,4,3,1,1,512]{5,4,2,1,3,0:T(2,128)(2,1)S(1)} collective-permute-done((bf16[2,4,3,1,1,512]{5,4,2,1,3,0:T(2,128)(2,1)S(1)}, bf16[2,4,3,1,1,512]{5,4,2,1,3,0:T(2,128)(2,1)S(1)}, u32[]{:S(2)}, u32[]{:S(2)}) %collective-permute-start.5) | collective-permute-done | bytes 24608 | tf_op jit(solution)/shard_map/ppermute | solution.py:30
  63.4 0.3 bitcast_convert_fusion
  63.7 0.9 copy-done.1
  64.6 1.9 %multiply_reduce_fusion.1 = f32[4,512,24]{1,0,2:T(4,128)} fusion(f32[4,512,3,2,4]{1,0,2,4,3:T(4,128)S(1)} %bitcast_convert_fusion, bf16[24,2,4,3,1,4,512]{6,5,4,3,2,1,0:T(4,128)(2,1)S(1)} %copy-done.1), kind=kLoop, calls=%fused_computation.1 | loop fusion | flops 3489792 | bytes 2752512
  66.5 1.3 copy.331
  67.8 1.8 %fusion = f32[32,24]{1,0:T(8,128)} fusion(f32[24,2048]{0,1:T(8,128)S(1)} %bitcast.1397, s32[2048]{0:T(1024)} %bitcast.1414), kind=kOutput, calls=%fused_computation.9 | convolution fusion | flops 18939904 | bytes 207872 | tf_op jit(solution)/shard_map/am,vm->av/dot_general | solution.py:161
  69.6 0.8 reshape.7026
  70.4 40.8 %psum.7 = f32[768]{0:T(1024)S(1)} all-reduce(f32[768]{0:T(1024)S(1)} %reshape.7026), channel_id=1, replica_groups=mesh['ta'=64,'gz'=16] {'gz'}, use_global_device_ids=true, to_apply=%region_0.1 | all-reduce | flops 768 | bytes 6144 | tf_op jit(solution)/shard_map/psum | solution.py:164
  111.2 0.2 convolution_bitcast_fusion
  111.4 0.2 dynamic-update-slice
  111.6 37.6 %all-reduce = bf16[768]{0:T(1024)(128)(2,1)S(1)} all-reduce(f32[768]{0:T(1024)S(1)} %dynamic-update-slice), channel_id=1, replica_groups=mesh['ta'=64,'gz'=16] {'gz'}, use_global_device_ids=true, to_apply=%add | all-reduce | flops 768 | bytes 4608
  149.2 0.1 reshape.7027
  149.3 0.9 convolution_convert_fusion
  150.3 1.3 multiply_reduce_fusion
  151.6 0.7 bitcast_add_fusion
  (317 shorter events, 7.7 us)
Async XLA Ops:
  0.0 111.2 %copy-start = (f32[1,48,768]{2,1,0:T(8,128)S(1)}, f32[1,48,768]{2,1,0:T(8,128)}, u32[]{:S(2)}) copy-start(f32[1,48,768]{2,1,0:T(8,128)} %param.11) | copy-start | bytes 442372
  1.9 35.8 %collective-permute-start.2 = (bf16[2,4,3,1,4,512]{5,4,2,3,1,0:T(4,128)(2,1)S(1)}, bf16[2,4,3,1,4,512]{5,4,2,3,1,0:T(4,128)(2,1)S(1)}, u32[]{:S(2)}, u32[]{:S(2)}) collective-permute-start(bf16[2,4,3,1,4,512]{5,4,2,3,1,0:T(4,128)(2,1)S(1)} %get-tuple-element.9), channel_id=1, source_target_pairs={{16,0},{32,16},{48,32},{64,48},{80,64},{96,80},{112,96},{128,112},... | collective-permute-start | bytes 294920 | tf_op jit(solution)/shard_map/ppermute | solution.py:30
  18.8 16.6 %collective-permute-start = (bf16[2,4,3,1,1,512]{5,4,2,3,1,0:T(2,128)(2,1)}, bf16[2,4,3,1,1,512]{5,4,2,3,1,0:T(2,128)(2,1)}, u32[]{:S(2)}, u32[]{:S(2)}) collective-permute-start(bf16[2,4,3,1,1,512]{5,4,2,3,1,0:T(2,128)(2,1)} %slice.2542), channel_id=1, source_target_pairs={{1,0},{2,1},{3,2},{4,3},{5,4},{6,5},{7,6},{8,7},{9,8},{10,9},{11,1... | collective-permute-start | bytes 73736 | tf_op jit(solution)/shard_map/ppermute | solution.py:30
  23.6 13.1 %collective-permute-start.1 = (bf16[2,4,3,1,1,512]{5,4,2,3,1,0:T(2,128)(2,1)}, bf16[2,4,3,1,1,512]{5,4,2,3,1,0:T(2,128)(2,1)}, u32[]{:S(2)}, u32[]{:S(2)}) collective-permute-start(bf16[2,4,3,1,1,512]{5,4,2,3,1,0:T(2,128)(2,1)} %fusion.38), channel_id=1, source_target_pairs={{15,0},{0,1},{1,2},{2,3},{3,4},{4,5},{5,6},{6,7},{7,8},{8,9},{9,10... | collective-permute-start | bytes 73736 | tf_op jit(solution)/shard_map/ppermute | solution.py:30
  27.6 10.5 %collective-permute-start.3 = (bf16[2,4,3,1,4,512]{5,4,2,3,1,0:T(4,128)(2,1)S(1)}, bf16[2,4,3,1,4,512]{5,4,2,3,1,0:T(4,128)(2,1)}, u32[]{:S(2)}, u32[]{:S(2)}) collective-permute-start(bf16[2,4,3,1,4,512]{5,4,2,3,1,0:T(4,128)(2,1)S(1)} %pad_maximum_fusion.7), channel_id=1, source_target_pairs={{1008,0},{0,16},{16,32},{32,48},{48,64},{64,80},{80,96},{96,112},{... | collective-permute-start | bytes 294920 | tf_op jit(solution)/shard_map/ppermute | solution.py:30
  30.6 1.2 copy-start.5
  36.6 2.5 %copy-start.4 = (bf16[2,4,3,1,4,512]{5,4,3,2,1,0:T(4,128)(2,1)S(1)}, bf16[2,4,3,1,4,512]{5,4,3,2,1,0:T(4,128)(2,1)}, u32[]{:S(2)}) copy-start(bf16[2,4,3,1,4,512]{5,4,3,2,1,0:T(4,128)(2,1)} %param.6) | copy-start | bytes 294916
  39.5 23.9 %copy-start.2 = (f32[2,4,3,1,4,512]{5,4,3,2,1,0:T(4,128)}, f32[2,4,3,1,4,512]{5,4,3,2,1,0:T(4,128)S(1)}, u32[]{:S(2)}) copy-start(f32[2,4,3,1,4,512]{5,4,3,2,1,0:T(4,128)S(1)} %get-tuple-element.7) | copy-start | bytes 589828
  40.8 1.5 %copy-start.6 = (f32[4,512]{1,0:T(4,128)S(1)}, f32[4,512]{1,0:T(4,128)}, u32[]{:S(2)}) copy-start(f32[4,512]{1,0:T(4,128)} %copy-done.5) | copy-start | bytes 24580
  44.0 18.6 %collective-permute-start.6 = (bf16[2,4,3,1,4,512]{5,4,3,2,1,0:T(4,128)(2,1)S(1)}, bf16[2,4,3,1,4,512]{5,4,3,2,1,0:T(4,128)(2,1)S(1)}, u32[]{:S(2)}, u32[]{:S(2)}) collective-permute-start(bf16[2,4,3,1,4,512]{5,4,3,2,1,0:T(4,128)(2,1)S(1)} %get-tuple-element.6), channel_id=1, source_target_pairs={{16,0},{32,16},{48,32},{64,48},{80,64},{96,80},{112,96},{128,112},... | collective-permute-start | bytes 294920 | tf_op jit(solution)/shard_map/ppermute | solution.py:30
  47.3 8.7 %collective-permute-start.4 = (bf16[2,4,3,1,1,512]{5,4,2,3,1,0:T(2,128)(2,1)S(1)}, bf16[2,4,3,1,1,512]{5,4,2,3,1,0:T(2,128)(2,1)S(1)}, u32[]{:S(2)}, u32[]{:S(2)}) collective-permute-start(bf16[2,4,3,1,1,512]{5,4,2,3,1,0:T(2,128)(2,1)S(1)} %slice.2726), channel_id=1, source_target_pairs={{1,0},{2,1},{3,2},{4,3},{5,4},{6,5},{7,6},{8,7},{9,8},{10,9},{11,1... | collective-permute-start | bytes 73736 | tf_op jit(solution)/shard_map/ppermute | solution.py:30
  53.1 9.3 %collective-permute-start.5 = (bf16[2,4,3,1,1,512]{5,4,2,1,3,0:T(2,128)(2,1)S(1)}, bf16[2,4,3,1,1,512]{5,4,2,1,3,0:T(2,128)(2,1)S(1)}, u32[]{:S(2)}, u32[]{:S(2)}) collective-permute-start(bf16[2,4,3,1,1,512]{5,4,2,1,3,0:T(2,128)(2,1)S(1)} %fusion.37), channel_id=1, source_target_pairs={{15,0},{0,1},{1,2},{2,3},{3,4},{4,5},{5,6},{6,7},{7,8},{8,9},{9,10... | collective-permute-start | bytes 73736 | tf_op jit(solution)/shard_map/ppermute | solution.py:30
  55.6 7.5 %collective-permute-start.7 = (bf16[2,4,3,1,4,512]{5,4,2,1,3,0:T(4,128)(2,1)S(1)}, bf16[2,4,3,1,4,512]{5,4,2,1,3,0:T(4,128)(2,1)S(1)}, u32[]{:S(2)}, u32[]{:S(2)}) collective-permute-start(bf16[2,4,3,1,4,512]{5,4,2,1,3,0:T(4,128)(2,1)S(1)} %pad_maximum_fusion.11), channel_id=1, source_target_pairs={{1008,0},{0,16},{16,32},{32,48},{48,64},{64,80},{80,96},{96,112},{... | collective-permute-start | bytes 294920 | tf_op jit(solution)/shard_map/ppermute | solution.py:30
  62.9 1.7 %copy-start.1 = (bf16[24,2,4,3,1,4,512]{6,5,4,3,2,1,0:T(4,128)(2,1)S(1)}, bf16[24,2,4,3,1,4,512]{6,5,4,3,2,1,0:T(4,128)(2,1)}, u32[]{:S(2)}) copy-start(bf16[24,2,4,3,1,4,512]{6,5,4,3,2,1,0:T(4,128)(2,1)} %param.10) | copy-start | bytes 7077892
  69.6 82.1 %copy-start.3 = (f32[2,4,3,1,4,512]{5,4,3,2,1,0:T(4,128)S(1)}, f32[2,4,3,1,4,512]{5,4,3,2,1,0:T(4,128)}, u32[]{:S(2)}) copy-start(f32[2,4,3,1,4,512]{5,4,3,2,1,0:T(4,128)} %copy-done.2) | copy-start | bytes 589828
where the time goes:
time: 153 us; the launch traced here: 152 us
  blocking collectives  78.4 us (51%)
  starting transfers between devices  32.8 us (21%)
  other arithmetic  18.4 us (12%)
  local copies, waits for them, and re-layouts  10.9 us (7%)
  waiting for transfers between devices  5.97 us (4%)
  between operations  3.08 us (2%)
  matrix products  2.86 us (2%)
    psum x1, blocking collectives, shards(): coarse_resid = lax.psum(partial_sum.reshape(-1), 'gz')  40.8 us
    unnamed x1, blocking collectives  37.6 us
    ppermute x8, starting transfers between devices, shifted(): return lax.ppermute(block, axis, route)  32.8 us
    ppermute x8, waiting for transfers between devices, shifted(): return lax.ppermute(block, axis, route)  5.97 us
    unnamed x18, local copies, waits for them, and re-layouts  3.75 us
  transfers between devices with their start and end apart: 8, of which 1 were waited for; matrix products, arithmetic and copies ran while one was open for 9% of the time, Pallas kernels for 0%

commit v1 on v0

--- a/solution.py
+++ b/solution.py
@@ -1,7 +1,7 @@
 import jax
 import jax.numpy as jnp
 from jax import lax
-from jax.sharding import PartitionSpec as P
+from jax.sharding import Mesh, PartitionSpec as P
 
 LX = 32
 LY = 16
@@ -24,8 +24,11 @@
 )
 
 
+GZ = ("gy", "gx")
+
+
 def shifted(block, axis, distance):
-    devices = range(lax.axis_size(axis))
+    devices = range(16 if axis == GZ else lax.axis_size(axis))
     route = [((i - distance) % len(devices), i) for i in devices]
     return lax.ppermute(block, axis, route)
 
@@ -116,9 +119,9 @@
     fwd_time = jnp.concatenate([spinor[:, :, :, 1:], ahead_time], axis=3)
     behind_time = shifted(send_bt, "ta", 1)
     bwd_time = jnp.concatenate([behind_time, send_bt[:, :, :, :-1]], axis=3)
-    ahead_space = shifted(spinor[:, :, :, :, 0:1], "gz", -1)
+    ahead_space = shifted(spinor[:, :, :, :, 0:1], GZ, -1)
     fwd_space = jnp.concatenate([spinor[:, :, :, :, 1:], ahead_space], axis=4)
-    behind_space = shifted(send_bz[:, :, :, :, -1:], "gz", 1)
+    behind_space = shifted(send_bz[:, :, :, :, -1:], GZ, 1)
     bwd_space = jnp.concatenate([behind_space, send_bz[:, :, :, :, :-1]], axis=4)
     fwd_space = fwd_round(fwd_space.astype(jnp.float32), 2)
     fwd_time = fwd_round(fwd_time.astype(jnp.float32), 3)
@@ -161,10 +164,14 @@
     partial_sum = jnp.einsum(
         "am,vm->av", member.astype(jnp.float32), projected.reshape(vectors, -1), precision=highest
     )
-    coarse_resid = lax.psum(partial_sum.reshape(-1), "gz")
+    coarse_resid = lax.psum(lax.psum(partial_sum.reshape(-1), "gx"), "gy")
     own_rows = jnp.dot(coarse_inverse[0], coarse_resid, precision=highest)
-    correction = lax.all_gather(own_rows, "gz", axis=0, tiled=True)
-    correction_half = correction.astype(jnp.bfloat16).reshape(NAGG, vectors)
+    rows = own_rows.shape[0]
+    place = (lax.axis_index("gy") * 4 + lax.axis_index("gx")) * rows
+    padded = lax.dynamic_update_slice(
+        jnp.zeros((rows * 16,), jnp.bfloat16), own_rows.astype(jnp.bfloat16), (place,)
+    )
+    correction_half = lax.psum(lax.psum(padded, "gx"), "gy").reshape(NAGG, vectors)
     spread = jnp.einsum(
         "av,am->vm",
         correction_half,
@@ -181,17 +188,19 @@
 
 
 def solution(mesh):
+    ta, gz = mesh.devices.shape
+    grid = Mesh(mesh.devices.reshape(ta, 4, gz // 4), ("ta", "gy", "gx"))
     return jax.shard_map(
         shards,
-        mesh=mesh,
+        mesh=grid,
         in_specs=(
-            P(None, None, None, "ta", "gz", None),
-            P(None, None, None, None, "ta", "gz", None),
-            P(None, None, "ta", "gz", None),
-            P("ta", "gz", None),
-            P(None, None, None, None, "ta", "gz", None),
-            P("ta", "gz", None),
+            P(None, None, None, "ta", GZ, None),
+            P(None, None, None, None, "ta", GZ, None),
+            P(None, None, "ta", GZ, None),
+            P("ta", GZ, None),
+            P(None, None, None, None, "ta", GZ, None),
+            P("ta", GZ, None),
         ),
-        out_specs=P(None, None, None, "ta", "gz", None),
+        out_specs=P(None, None, None, "ta", GZ, None),
         check_vma=False,
     )

time: 153 us -> 112 us (0.73)
  the two profiles are of different devices: /device:TPU:2 before, /device:TPU:10 now
where the time goes in v1:
time: 112 us
  blocking collectives  43.3 us (39%)
  starting transfers between devices  31.1 us (28%)
  other arithmetic  18.4 us (16%)
  local copies, waits for them, and re-layouts  9.66 us (9%)
  waiting for transfers between devices  3.91 us (3%)
  matrix products  2.87 us (3%)
  between operations  2.44 us (2%)
    ppermute x8, starting transfers between devices, shifted(): return lax.ppermute(block, axis, route)  31.1 us
    psum x2, blocking collectives, shards(): coarse_resid = lax.psum(lax.psum(partial_sum.reshape(-1), 'gx'), 'gy')  25 us
    psum x1, blocking collectives, shards(): lax.psum(lax.psum(padded, 'gx'), 'gy').reshape(NAGG, vectors)  10.6 us
    psum x1, blocking collectives, shards(): lax.psum(padded, 'gx')  7.72 us
    ppermute x8, waiting for transfers between devices, shifted(): return lax.ppermute(block, axis, route)  3.91 us
    unnamed x3, other arithmetic  2.27 us
  transfers between devices with their start and end apart: 8, of which 1 were waited for; matrix products, arithmetic and copies ran while one was open for 12% of the time, Pallas kernels for 0%

profile of v1, /device:TPU:10, one launch (start us, length us, event | category | flops | bytes accessed | tf_op | source)
XLA Modules:
  0.0 111.6 jit_solution(6722427594549624277)
XLA Ops:
  0.0 1.0 add_bitcast_fusion
  1.0 1.0 fusion.281
  1.9 16.2 %collective-permute-start.2 = (bf16[2,4,3,1,4,512]{5,4,2,3,1,0:T(4,128)(2,1)S(1)}, bf16[2,4,3,1,4,512]{5,4,2,3,1,0:T(4,128)(2,1)S(1)}, u32[]{:S(2)}, u32[]{:S(2)}) collective-permute-start(bf16[2,4,3,1,4,512]{5,4,2,3,1,0:T(4,128)(2,1)S(1)} %get-tuple-element.9), channel_id=1, source_target_pairs={{16,0},{32,16},{48,32},{64,48},{80,64},{96,80},{112,96},{128,112},... | collective-permute-start | bytes 294920 | tf_op jit(solution)/shard_map/ppermute | solution.py:33
  18.1 0.7 slice.2542
  18.8 2.4 %collective-permute-start = (bf16[2,4,3,1,1,512]{5,4,2,3,1,0:T(2,128)(2,1)}, bf16[2,4,3,1,1,512]{5,4,2,3,1,0:T(2,128)(2,1)}, u32[]{:S(2)}, u32[]{:S(2)}) collective-permute-start(bf16[2,4,3,1,1,512]{5,4,2,3,1,0:T(2,128)(2,1)} %slice.2542), channel_id=1, source_target_pairs={{1,0},{2,1},{3,2},{4,3},{5,4},{6,5},{7,6},{8,7},{9,8},{10,9},{11,1... | collective-permute-start | bytes 73736 | tf_op jit(solution)/shard_map/ppermute | solution.py:33
  21.3 0.9 bitcast_convert_fusion.9
  22.9 0.7 fusion.39
  23.6 3.4 %collective-permute-start.1 = (bf16[2,4,3,1,1,512]{5,4,2,3,1,0:T(2,128)(2,1)}, bf16[2,4,3,1,1,512]{5,4,2,3,1,0:T(2,128)(2,1)}, u32[]{:S(2)}, u32[]{:S(2)}) collective-permute-start(bf16[2,4,3,1,1,512]{5,4,2,3,1,0:T(2,128)(2,1)} %fusion.39), channel_id=1, source_target_pairs={{15,0},{0,1},{1,2},{2,3},{3,4},{4,5},{5,6},{6,7},{7,8},{8,9},{9,10... | collective-permute-start | bytes 73736 | tf_op jit(solution)/shard_map/ppermute | solution.py:33
  27.8 0.2 reshape.7015
  27.9 0.1 slice.1197
  28.1 0.1 fusion.32
  28.2 0.1 reshape.7030
  28.3 0.1 reshape.7032
  29.2 0.2 reshape.7016
  29.3 0.1 slice.1244
  29.4 0.1 maximum_convert_fusion
  29.6 0.2 reshape.7035
  29.9 0.2 reshape.7017
  30.3 0.1 reshape.7037
  30.4 0.1 reshape.7039
  31.2 0.2 reshape.7018
  31.5 0.2 reshape.7040
  32.2 1.3 %copy.342 = s32[1,4,4,128]{3,1,2,0:T(4,128)} copy(s32[1,4,4,128]{3,2,1,0:T(4,128)} %bitcast.1417) | data formatting | bytes 16384
  33.5 0.9 maximum_convert_fusion.4
  34.8 0.8 fusion.43
  36.2 0.8 slice_convert_fusion.1
  37.2 0.3 bitcast_convert_fusion.10
  37.7 0.2 reshape.7019
  37.9 0.1 slice.2661
  38.0 0.1 fusion.28
  38.1 0.1 reshape.7061
  38.3 0.1 reshape.7062
  39.0 0.2 reshape.7020
  39.2 0.1 slice.2691
  39.3 0.1 maximum_convert_fusion.2
  39.4 0.2 reshape.7065
  39.8 0.2 reshape.7021
  40.1 0.1 reshape.7066
  40.3 0.1 reshape.7067
  41.1 0.2 reshape.7022
  41.2 0.1 maximum_convert_fusion.3
  41.3 0.2 reshape.7068
  42.1 2.9 %collective-permute-start.6 = (bf16[2,4,3,1,4,512]{5,4,3,2,1,0:T(4,128)(2,1)S(1)}, bf16[2,4,3,1,4,512]{5,4,3,2,1,0:T(4,128)(2,1)S(1)}, u32[]{:S(2)}, u32[]{:S(2)}) collective-permute-start(bf16[2,4,3,1,4,512]{5,4,3,2,1,0:T(4,128)(2,1)S(1)} %get-tuple-element.6), channel_id=1, source_target_pairs={{16,0},{32,16},{48,32},{64,48},{80,64},{96,80},{112,96},{128,112},... | collective-permute-start | bytes 294920 | tf_op jit(solution)/shard_map/ppermute | solution.py:33
  45.3 3.1 %collective-permute-start.4 = (bf16[2,4,3,1,1,512]{5,4,2,3,1,0:T(2,128)(2,1)S(1)}, bf16[2,4,3,1,1,512]{5,4,2,3,1,0:T(2,128)(2,1)S(1)}, u32[]{:S(2)}, u32[]{:S(2)}) collective-permute-start(bf16[2,4,3,1,1,512]{5,4,2,3,1,0:T(2,128)(2,1)S(1)} %slice.2726), channel_id=1, source_target_pairs={{1,0},{2,1},{3,2},{4,3},{5,4},{6,5},{7,6},{8,7},{9,8},{10,9},{11,1... | collective-permute-start | bytes 73736 | tf_op jit(solution)/shard_map/ppermute | solution.py:33
  48.5 0.1 fusion.38
  48.6 2.9 %collective-permute-start.5 = (bf16[2,4,3,1,1,512]{5,4,2,1,3,0:T(2,128)(2,1)S(1)}, bf16[2,4,3,1,1,512]{5,4,2,1,3,0:T(2,128)(2,1)S(1)}, u32[]{:S(2)}, u32[]{:S(2)}) collective-permute-start(bf16[2,4,3,1,1,512]{5,4,2,1,3,0:T(2,128)(2,1)S(1)} %fusion.38), channel_id=1, source_target_pairs={{15,0},{0,1},{1,2},{2,3},{3,4},{4,5},{5,6},{6,7},{7,8},{8,9},{9,10... | collective-permute-start | bytes 73736 | tf_op jit(solution)/shard_map/ppermute | solution.py:33
  52.3 0.1 maximum_convert_fusion.5
  52.8 3.9 %collective-permute-done.5 = bf16[2,4,3,1,1,512]{5,4,2,1,3,0:T(2,128)(2,1)S(1)} collective-permute-done((bf16[2,4,3,1,1,512]{5,4,2,1,3,0:T(2,128)(2,1)S(1)}, bf16[2,4,3,1,1,512]{5,4,2,1,3,0:T(2,128)(2,1)S(1)}, u32[]{:S(2)}, u32[]{:S(2)}) %collective-permute-start.5) | collective-permute-done | bytes 24608 | tf_op jit(solution)/shard_map/ppermute | solution.py:33
  57.6 0.3 bitcast_convert_fusion
  58.0 0.9 copy-done.1
  58.8 1.9 %multiply_reduce_fusion.1 = f32[4,512,24]{1,0,2:T(4,128)} fusion(f32[4,512,3,2,4]{1,0,2,4,3:T(4,128)S(1)} %bitcast_convert_fusion, bf16[24,2,4,3,1,4,512]{6,5,4,3,2,1,0:T(4,128)(2,1)S(1)} %copy-done.1), kind=kLoop, calls=%fused_computation.1 | loop fusion | flops 3489792 | bytes 2752512
  60.8 1.3 %copy.331 = f32[4,512,24]{2,1,0:T(8,128)S(1)} copy(f32[4,512,24]{1,0,2:T(4,128)} %multiply_reduce_fusion.1) | data formatting | bytes 393216 | tf_op jit(solution)/shard_map/vrsctzn,rsctzn->vtzn/dot_general | solution.py:158
  62.1 1.8 %fusion.1 = f32[32,24]{1,0:T(8,128)} fusion(f32[24,2048]{0,1:T(8,128)S(1)} %bitcast.1398, s32[2048]{0:T(1024)} %bitcast.1415), kind=kOutput, calls=%fused_computation.10 | convolution fusion | flops 18939904 | bytes 207872 | tf_op jit(solution)/shard_map/am,vm->av/dot_general | solution.py:164
  63.9 0.8 reshape.7026
  64.7 11.9 %psum.28 = f32[768]{0:T(1024)S(1)} all-reduce(f32[768]{0:T(1024)S(1)} %reshape.7026), channel_id=1, replica_groups=mesh['ta'=64,'gy'=4,'gx'=4] {'gx'}, use_global_device_ids=true, to_apply=%region_0.1 | all-reduce | flops 768 | bytes 6144 | tf_op jit(solution)/shard_map/psum | solution.py:167
  76.6 13.2 %psum.29 = f32[768]{0:T(1024)S(1)} all-reduce(f32[768]{0:T(1024)S(1)} %psum.28), channel_id=1, replica_groups=mesh['ta'=64,'gy'=4,'gx'=4] {'gy'}, use_global_device_ids=true, to_apply=%region_1.2 | all-reduce | flops 768 | bytes 6144 | tf_op jit(solution)/shard_map/psum | solution.py:167
  89.7 0.2 fusion
  89.9 0.3 dynamic_update_slice.3
  90.2 7.7 %psum.30 = bf16[768]{0:T(1024)(128)(2,1)S(1)} all-reduce(bf16[768]{0:T(1024)(128)(2,1)S(1)} %dynamic_update_slice.3), channel_id=1, replica_groups=mesh['ta'=64,'gy'=4,'gx'=4] {'gx'}, use_global_device_ids=true, to_apply=%region_2.3 | all-reduce | flops 768 | bytes 3072 | tf_op jit(solution)/shard_map/psum | solution.py:174
  97.9 0.1 reshape.7027
  98.0 10.6 %psum.31 = bf16[32,24]{1,0:T(8,128)(2,1)S(1)} all-reduce(bf16[32,24]{1,0:T(8,128)(2,1)S(1)} %reshape.7027), channel_id=1, replica_groups=mesh['ta'=64,'gy'=4,'gx'=4] {'gy'}, use_global_device_ids=true, to_apply=%region_3.4 | all-reduce | flops 768 | bytes 3072 | tf_op jit(solution)/shard_map/psum | solution.py:174
  108.6 0.9 convolution_convert_fusion
  109.6 1.3 %multiply_reduce_fusion = f32[4,512,2,4,3]{1,0,4,3,2:T(4,128)S(1)} fusion(f32[4,512,24]{1,0,2:T(4,128)S(1)} %bitcast_convert_fusion.1, bf16[24,2,4,3,1,4,512]{6,5,4,3,2,1,0:T(4,128)(2,1)S(1)} %copy-done.1), kind=kLoop, calls=%fused_computation | loop fusion | flops 3489792 | bytes 2752512 | tf_op jit(solution)/shard_map/vrsctzn,vtzn->rsctzn/dot_general | solution.py:181
  110.9 0.7 bitcast_add_fusion
  (318 shorter events, 7.8 us)
Async XLA Ops:
  0.0 89.7 %copy-start = (f32[1,48,768]{2,1,0:T(8,128)S(1)}, f32[1,48,768]{2,1,0:T(8,128)}, u32[]{:S(2)}) copy-start(f32[1,48,768]{2,1,0:T(8,128)} %param.11) | copy-start | bytes 442372
  1.9 33.8 %collective-permute-start.2 = (bf16[2,4,3,1,4,512]{5,4,2,3,1,0:T(4,128)(2,1)S(1)}, bf16[2,4,3,1,4,512]{5,4,2,3,1,0:T(4,128)(2,1)S(1)}, u32[]{:S(2)}, u32[]{:S(2)}) collective-permute-start(bf16[2,4,3,1,4,512]{5,4,2,3,1,0:T(4,128)(2,1)S(1)} %get-tuple-element.9), channel_id=1, source_target_pairs={{16,0},{32,16},{48,32},{64,48},{80,64},{96,80},{112,96},{128,112},... | collective-permute-start | bytes 294920 | tf_op jit(solution)/shard_map/ppermute | solution.py:33
  18.8 14.7 %collective-permute-start = (bf16[2,4,3,1,1,512]{5,4,2,3,1,0:T(2,128)(2,1)}, bf16[2,4,3,1,1,512]{5,4,2,3,1,0:T(2,128)(2,1)}, u32[]{:S(2)}, u32[]{:S(2)}) collective-permute-start(bf16[2,4,3,1,1,512]{5,4,2,3,1,0:T(2,128)(2,1)} %slice.2542), channel_id=1, source_target_pairs={{1,0},{2,1},{3,2},{4,3},{5,4},{6,5},{7,6},{8,7},{9,8},{10,9},{11,1... | collective-permute-start | bytes 73736 | tf_op jit(solution)/shard_map/ppermute | solution.py:33
  23.6 11.2 %collective-permute-start.1 = (bf16[2,4,3,1,1,512]{5,4,2,3,1,0:T(2,128)(2,1)}, bf16[2,4,3,1,1,512]{5,4,2,3,1,0:T(2,128)(2,1)}, u32[]{:S(2)}, u32[]{:S(2)}) collective-permute-start(bf16[2,4,3,1,1,512]{5,4,2,3,1,0:T(2,128)(2,1)} %fusion.39), channel_id=1, source_target_pairs={{15,0},{0,1},{1,2},{2,3},{3,4},{4,5},{5,6},{6,7},{7,8},{8,9},{9,10... | collective-permute-start | bytes 73736 | tf_op jit(solution)/shard_map/ppermute | solution.py:33
  27.6 8.6 %collective-permute-start.3 = (bf16[2,4,3,1,4,512]{5,4,2,3,1,0:T(4,128)(2,1)S(1)}, bf16[2,4,3,1,4,512]{5,4,2,3,1,0:T(4,128)(2,1)}, u32[]{:S(2)}, u32[]{:S(2)}) collective-permute-start(bf16[2,4,3,1,4,512]{5,4,2,3,1,0:T(4,128)(2,1)S(1)} %pad_maximum_fusion.7), channel_id=1, source_target_pairs={{1008,0},{0,16},{16,32},{32,48},{48,64},{64,80},{80,96},{96,112},{... | collective-permute-start | bytes 294920 | tf_op jit(solution)/shard_map/ppermute | solution.py:33
  30.6 1.2 %copy-start.5 = (f32[4,512]{1,0:T(4,128)}, f32[4,512]{1,0:T(4,128)S(1)}, u32[]{:S(2)}) copy-start(f32[4,512]{1,0:T(4,128)S(1)} %get-tuple-element.277) | copy-start | bytes 24580
  34.7 2.5 %copy-start.4 = (bf16[2,4,3,1,4,512]{5,4,3,2,1,0:T(4,128)(2,1)S(1)}, bf16[2,4,3,1,4,512]{5,4,3,2,1,0:T(4,128)(2,1)}, u32[]{:S(2)}) copy-start(bf16[2,4,3,1,4,512]{5,4,3,2,1,0:T(4,128)(2,1)} %param.6) | copy-start | bytes 294916
  37.5 20.1 %copy-start.2 = (f32[2,4,3,1,4,512]{5,4,3,2,1,0:T(4,128)}, f32[2,4,3,1,4,512]{5,4,3,2,1,0:T(4,128)S(1)}, u32[]{:S(2)}) copy-start(f32[2,4,3,1,4,512]{5,4,3,2,1,0:T(4,128)S(1)} %get-tuple-element.7) | copy-start | bytes 589828
  38.9 1.5 %copy-start.6 = (f32[4,512]{1,0:T(4,128)S(1)}, f32[4,512]{1,0:T(4,128)}, u32[]{:S(2)}) copy-start(f32[4,512]{1,0:T(4,128)} %copy-done.5) | copy-start | bytes 24580
  42.1 14.9 %collective-permute-start.6 = (bf16[2,4,3,1,4,512]{5,4,3,2,1,0:T(4,128)(2,1)S(1)}, bf16[2,4,3,1,4,512]{5,4,3,2,1,0:T(4,128)(2,1)S(1)}, u32[]{:S(2)}, u32[]{:S(2)}) collective-permute-start(bf16[2,4,3,1,4,512]{5,4,3,2,1,0:T(4,128)(2,1)S(1)} %get-tuple-element.6), channel_id=1, source_target_pairs={{16,0},{32,16},{48,32},{64,48},{80,64},{96,80},{112,96},{128,112},... | collective-permute-start | bytes 294920 | tf_op jit(solution)/shard_map/ppermute | solution.py:33
  45.3 7.0 %collective-permute-start.4 = (bf16[2,4,3,1,1,512]{5,4,2,3,1,0:T(2,128)(2,1)S(1)}, bf16[2,4,3,1,1,512]{5,4,2,3,1,0:T(2,128)(2,1)S(1)}, u32[]{:S(2)}, u32[]{:S(2)}) collective-permute-start(bf16[2,4,3,1,1,512]{5,4,2,3,1,0:T(2,128)(2,1)S(1)} %slice.2726), channel_id=1, source_target_pairs={{1,0},{2,1},{3,2},{4,3},{5,4},{6,5},{7,6},{8,7},{9,8},{10,9},{11,1... | collective-permute-start | bytes 73736 | tf_op jit(solution)/shard_map/ppermute | solution.py:33
  48.6 8.1 %collective-permute-start.5 = (bf16[2,4,3,1,1,512]{5,4,2,1,3,0:T(2,128)(2,1)S(1)}, bf16[2,4,3,1,1,512]{5,4,2,1,3,0:T(2,128)(2,1)S(1)}, u32[]{:S(2)}, u32[]{:S(2)}) collective-permute-start(bf16[2,4,3,1,1,512]{5,4,2,1,3,0:T(2,128)(2,1)S(1)} %fusion.38), channel_id=1, source_target_pairs={{15,0},{0,1},{1,2},{2,3},{3,4},{4,5},{5,6},{6,7},{7,8},{8,9},{9,10... | collective-permute-start | bytes 73736 | tf_op jit(solution)/shard_map/ppermute | solution.py:33
  52.0 5.5 %collective-permute-start.7 = (bf16[2,4,3,1,4,512]{5,4,2,1,3,0:T(4,128)(2,1)S(1)}, bf16[2,4,3,1,4,512]{5,4,2,1,3,0:T(4,128)(2,1)S(1)}, u32[]{:S(2)}, u32[]{:S(2)}) collective-permute-start(bf16[2,4,3,1,4,512]{5,4,2,1,3,0:T(4,128)(2,1)S(1)} %pad_maximum_fusion.11), channel_id=1, source_target_pairs={{1008,0},{0,16},{16,32},{32,48},{48,64},{64,80},{80,96},{96,112},{... | collective-permute-start | bytes 294920 | tf_op jit(solution)/shard_map/ppermute | solution.py:33
  57.2 1.7 %copy-start.1 = (bf16[24,2,4,3,1,4,512]{6,5,4,3,2,1,0:T(4,128)(2,1)S(1)}, bf16[24,2,4,3,1,4,512]{6,5,4,3,2,1,0:T(4,128)(2,1)}, u32[]{:S(2)}) copy-start(bf16[24,2,4,3,1,4,512]{6,5,4,3,2,1,0:T(4,128)(2,1)} %param.10) | copy-start | bytes 7077892
  63.9 47.0 %copy-start.3 = (f32[2,4,3,1,4,512]{5,4,3,2,1,0:T(4,128)S(1)}, f32[2,4,3,1,4,512]{5,4,3,2,1,0:T(4,128)}, u32[]{:S(2)}) copy-start(f32[2,4,3,1,4,512]{5,4,3,2,1,0:T(4,128)} %copy-done.2) | copy-start | bytes 589828

commit v2 on v1

--- a/solution.py
+++ b/solution.py
@@ -94,53 +94,44 @@
 
 
 def local_shift(values, direction, step):
-    dims_all = values.shape
-    grid = values.reshape(dims_all[:-1] + (LY, LX))
-    rolled = jnp.roll(grid, -step, axis=-1 if direction == 0 else -2)
-    return rolled.reshape(dims_all)
+    if direction == 1:
+        return jnp.roll(values, -step * LX, axis=-1)
+    column = lax.broadcasted_iota(jnp.int32, values.shape, values.ndim - 1) % LX
+    edge = LX - 1 if step > 0 else 0
+    return jnp.where(
+        column == edge,
+        jnp.roll(values, step * (LX - 1), axis=-1),
+        jnp.roll(values, -step, axis=-1),
+    )
 
 
-def fwd_round(wide, direction):
-    return lax.optimization_barrier(project(wide, direction, -1.0).astype(jnp.bfloat16))
+def halo(block, axis, dim, step):
+    size = block.shape[dim]
+    if step > 0:
+        edge = lax.slice_in_dim(block, 0, 1, axis=dim)
+        inner = lax.slice_in_dim(block, 1, size, axis=dim)
+        return jnp.concatenate([inner, shifted(edge, axis, -1)], axis=dim)
+    edge = lax.slice_in_dim(block, size - 1, size, axis=dim)
+    inner = lax.slice_in_dim(block, 0, size - 1, axis=dim)
+    return jnp.concatenate([shifted(edge, axis, 1), inner], axis=dim)
 
 
 def hopping(spinor, gauge_links):
     wide = spinor.astype(jnp.float32)
-    total = jnp.zeros(spinor.shape, jnp.float32)
-    back_space = lax.optimization_barrier(
-        project(color_mix(gauge_links[2], spinor, True), 2, 1.0).astype(jnp.bfloat16)
-    )
-    back_time = lax.optimization_barrier(
-        project(color_mix(gauge_links[3], spinor, True), 3, 1.0).astype(jnp.bfloat16)
-    )
-    send_bz = expand(back_space.astype(jnp.float32), 2, 1.0).astype(jnp.bfloat16)
-    send_bt = expand(back_time.astype(jnp.float32), 3, 1.0).astype(jnp.bfloat16)
-    ahead_time = shifted(spinor, "ta", -1)
-    fwd_time = jnp.concatenate([spinor[:, :, :, 1:], ahead_time], axis=3)
-    behind_time = shifted(send_bt, "ta", 1)
-    bwd_time = jnp.concatenate([behind_time, send_bt[:, :, :, :-1]], axis=3)
-    ahead_space = shifted(spinor[:, :, :, :, 0:1], GZ, -1)
-    fwd_space = jnp.concatenate([spinor[:, :, :, :, 1:], ahead_space], axis=4)
-    behind_space = shifted(send_bz[:, :, :, :, -1:], GZ, 1)
-    bwd_space = jnp.concatenate([behind_space, send_bz[:, :, :, :, :-1]], axis=4)
-    fwd_space = fwd_round(fwd_space.astype(jnp.float32), 2)
-    fwd_time = fwd_round(fwd_time.astype(jnp.float32), 3)
-    bwd_space = bwd_space[:, 0:2]
-    bwd_time = bwd_time[:, 0:2]
-    for direction in range(2):
-        ahead = local_shift(fwd_round(wide, direction), direction, 1)
-        total = total + expand(color_mix(gauge_links[direction], ahead, False), direction, -1.0)
-        back_half = lax.optimization_barrier(
-            project(color_mix(gauge_links[direction], spinor, True), direction, 1.0).astype(
-                jnp.bfloat16
-            )
-        )
-        behind = local_shift(back_half, direction, -1).astype(jnp.float32)
-        total = total + expand(behind, direction, 1.0)
-    total = total + expand(color_mix(gauge_links[2], fwd_space, False), 2, -1.0)
-    total = total + expand(bwd_space.astype(jnp.float32), 2, 1.0)
-    total = total + expand(color_mix(gauge_links[3], fwd_time, False), 3, -1.0)
-    total = total + expand(bwd_time.astype(jnp.float32), 3, 1.0)
+    fwd = [project(wide, mu, -1.0).astype(jnp.bfloat16) for mu in range(4)]
+    back = [
+        project(color_mix(gauge_links[mu], spinor, True), mu, 1.0).astype(jnp.bfloat16)
+        for mu in range(4)
+    ]
+    ahead = [local_shift(fwd[0], 0, 1), local_shift(fwd[1], 1, 1)]
+    behind = [local_shift(back[0], 0, -1), local_shift(back[1], 1, -1)]
+    ahead += [halo(fwd[2], GZ, 4, 1), halo(fwd[3], "ta", 3, 1)]
+    behind += [halo(back[2], GZ, 4, -1), halo(back[3], "ta", 3, -1)]
+    total = None
+    for mu in range(4):
+        term = expand(color_mix(gauge_links[mu], ahead[mu], False), mu, -1.0)
+        term = term + expand(behind[mu].astype(jnp.float32), mu, 1.0)
+        total = term if total is None else total + term
     return total
 
 

time: 112 us -> 102 us (0.911)
  local copies, waits for them, and re-layouts: 9.66 us -> 3.45 us
  other arithmetic: 18.4 us -> 15.2 us
  starting transfers between devices: 31.1 us -> 29.4 us
    convert_element_type x15 -> x8, other arithmetic: 3.22 us -> 0.46 us  [the longest x7 0.45 us: hopping(): term = term + expand(behind[mu].astype(jnp.float32), mu, 1.0)]
    convert_element_type x12 -> x0, local copies, waits for them, and re-layouts: 1.85 us -> none  [the longest x4 0.77 us: hopping(): behind = local_shift(back_half, direction, -1).astype(jnp.float32)]
    ppermute x8, starting transfers between devices: 31.1 us -> 29.4 us  [shifted(): return lax.ppermute(block, axis, route)]
    unnamed x15 -> x13, local copies, waits for them, and re-layouts: 2.21 us -> 0.63 us
    slice x14 -> x0, local copies, waits for them, and re-layouts: 1.5 us -> none  [the longest x10 0.7 us: local_shift(): rolled = jnp.roll(grid, -step, axis=-1 if direction == 0 else -2)]
    psum x1, blocking collectives: 7.72 us -> 9.07 us  [shards(): lax.psum(padded, 'gx')]
    another operation x38 -> x29, other arithmetic: 1.99 us -> 0.75 us  [expand(): return jnp.stack([jnp.stack(rows_re), jnp.stack(rows_im)])]
    reshape x8 -> x0, local copies, waits for them, and re-layouts: 1.22 us -> none  [local_shift(): grid = values.reshape(dims_all[:-1] + (LY, LX))]
  transfers between devices with their start and end apart: 8 -> 8, of which waited for: 1 -> 3; matrix products, arithmetic and copies ran while one was open for 12% -> 7% of each run, Pallas kernels for 0% -> 0%
where the time goes in v2:
time: 102 us; the launch traced here: 101 us
  blocking collectives  44.4 us (44%)
  starting transfers between devices  29.4 us (29%)
  other arithmetic  15.2 us (15%)
  waiting for transfers between devices  3.96 us (4%)
  local copies, waits for them, and re-layouts  3.45 us (3%)
  matrix products  2.86 us (3%)
  between operations  2.18 us (2%)
    ppermute x8, starting transfers between devices, shifted(): return lax.ppermute(block, axis, route)  29.4 us
    psum x2, blocking collectives, shards(): coarse_resid = lax.psum(lax.psum(partial_sum.reshape(-1), 'gx'), 'gy')  24.3 us
    psum x1, blocking collectives, shards(): lax.psum(lax.psum(padded, 'gx'), 'gy').reshape(NAGG, vectors)  11.1 us
    psum x1, blocking collectives, shards(): lax.psum(padded, 'gx')  9.07 us
    ppermute x8, waiting for transfers between devices, shifted(): return lax.ppermute(block, axis, route)  3.96 us
    unnamed x3, other arithmetic  2.27 us
    another operation x52, other arithmetic, project(): return jnp.stack([jnp.stack(rows_re), jnp.stack(rows_im)])  2.18 us
  transfers between devices with their start and end apart: 8, of which 3 were waited for; matrix products, arithmetic and copies ran while one was open for 7% of the time, Pallas kernels for 0%

profile of v2, /device:TPU:10, one launch (start us, length us, event | category | flops | bytes accessed | tf_op | source)
XLA Modules:
  0.0 101.5 jit_solution(16665423099628692793)
XLA Ops:
  0.0 1.0 add_bitcast_fusion
  1.0 1.0 fusion.267
  2.1 2.4 %collective-permute-start = (bf16[2,2,3,1,1,512]{5,4,2,1,3,0:T(2,128)(2,1)S(1)}, bf16[2,2,3,1,1,512]{5,4,2,1,3,0:T(2,128)(2,1)S(1)}, u32[]{:S(2)}, u32[]{:S(2)}) collective-permute-start(bf16[2,2,3,1,1,512]{5,4,2,1,3,0:T(2,128)(2,1)S(1)} %pad_maximum_fusion.33), channel_id=1, source_target_pairs={{1,0},{2,1},{3,2},{4,3},{5,4},{6,5},{7,6},{8,7},{9,8},{10,9},{11,1... | collective-permute-start | bytes 36872 | tf_op jit(solution)/shard_map/ppermute | solution.py:33
  4.5 0.9 bitcast_convert_fusion.10
  5.6 0.1 add_add_fusion.17
  5.7 0.1 add_add_fusion.16
  5.7 0.1 add_add_fusion.15
  6.0 3.4 %collective-permute-start.1 = (bf16[2,2,3,1,1,512]{5,4,2,1,3,0:T(2,128)(2,1)S(1)}, bf16[2,2,3,1,1,512]{5,4,2,1,3,0:T(2,128)(2,1)S(1)}, u32[]{:S(2)}, u32[]{:S(2)}) collective-permute-start(bf16[2,2,3,1,1,512]{5,4,2,1,3,0:T(2,128)(2,1)S(1)} %fusion.65), channel_id=1, source_target_pairs={{15,0},{0,1},{1,2},{2,3},{3,4},{4,5},{5,6},{6,7},{7,8},{8,9},{9,10... | collective-permute-start | bytes 36872 | tf_op jit(solution)/shard_map/ppermute | solution.py:33
  9.5 15.7 %collective-permute-start.2 = (bf16[2,2,3,1,4,512]{5,4,2,1,3,0:T(4,128)(2,1)S(1)}, bf16[2,2,3,1,4,512]{5,4,2,1,3,0:T(4,128)(2,1)S(1)}, u32[]{:S(2)}, u32[]{:S(2)}) collective-permute-start(bf16[2,2,3,1,4,512]{5,4,2,1,3,0:T(4,128)(2,1)S(1)} %pad_maximum_fusion.21), channel_id=1, source_target_pairs={{16,0},{32,16},{48,32},{64,48},{80,64},{96,80},{112,96},{128,112},... | collective-permute-start | bytes 147464 | tf_op jit(solution)/shard_map/ppermute | solution.py:33
  25.2 0.1 subtract_add_fusion.14
  25.3 0.1 subtract_add_fusion.13
  25.3 0.1 subtract_add_fusion.12
  25.8 0.1 fusion.27
  25.9 0.1 fusion.186
  26.0 0.1 fusion.21
  26.4 0.1 add_add_fusion.23
  26.5 0.1 add_add_fusion.22
  26.5 0.1 add_add_fusion.21
  26.8 0.1 fusion.184
  26.9 0.1 fusion.26
  27.0 0.1 fusion.30
  27.2 0.1 slice_maximum_fusion.3
  27.3 0.1 fusion.44
  27.6 0.1 subtract_add_fusion.20
  27.7 0.1 subtract_add_fusion.19
  27.7 0.1 subtract_add_fusion.18
  28.0 0.1 fusion.265
  28.5 0.6 copy.318
  29.4 0.1 fusion.41
  30.0 0.3 collective-permute-done.3
  30.5 0.3 bitcast_convert_fusion.1
  30.9 0.1 add_add_fusion.11
  31.0 0.1 add_add_fusion.10
  31.0 0.1 add_add_fusion.9
  31.3 0.1 fusion.23
  31.4 0.1 fusion.181
  31.7 0.1 fusion.24
  31.8 0.1 fusion.183
  31.9 0.2 fusion.20
  32.4 0.1 slice_maximum_fusion.1
  32.5 0.1 fusion.35
  32.8 0.1 subtract_add_fusion.8
  33.2 0.1 fusion.34
  33.6 0.1 subtract_add_fusion.1
  33.9 3.4 %collective-permute-start.4 = (bf16[2,2,3,1,1,512]{5,4,2,1,3,0:T(2,128)(2,1)S(1)}, bf16[2,2,3,1,1,512]{5,4,2,1,3,0:T(2,128)(2,1)S(1)}, u32[]{:S(2)}, u32[]{:S(2)}) collective-permute-start(bf16[2,2,3,1,1,512]{5,4,2,1,3,0:T(2,128)(2,1)S(1)} %pad_maximum_fusion.31), channel_id=1, source_target_pairs={{1,0},{2,1},{3,2},{4,3},{5,4},{6,5},{7,6},{8,7},{9,8},{10,9},{11,1... | collective-permute-start | bytes 36872 | tf_op jit(solution)/shard_map/ppermute | solution.py:33
  37.5 2.5 %collective-permute-start.5 = (bf16[2,2,3,1,1,512]{5,4,2,3,1,0:T(2,128)(2,1)S(1)}, bf16[2,2,3,1,1,512]{5,4,2,3,1,0:T(2,128)(2,1)S(1)}, u32[]{:S(2)}, u32[]{:S(2)}) collective-permute-start(bf16[2,2,3,1,1,512]{5,4,2,3,1,0:T(2,128)(2,1)S(1)} %fusion.61), channel_id=1, source_target_pairs={{15,0},{0,1},{1,2},{2,3},{3,4},{4,5},{5,6},{6,7},{7,8},{8,9},{9,10... | collective-permute-start | bytes 36872 | tf_op jit(solution)/shard_map/ppermute | solution.py:33
  40.1 2.1 %collective-permute-start.6 = (bf16[2,2,3,1,4,512]{5,4,2,1,3,0:T(4,128)(2,1)S(1)}, bf16[2,2,3,1,4,512]{5,4,2,1,3,0:T(4,128)(2,1)S(1)}, u32[]{:S(2)}, u32[]{:S(2)}) collective-permute-start(bf16[2,2,3,1,4,512]{5,4,2,1,3,0:T(4,128)(2,1)S(1)} %pad_maximum_fusion.28), channel_id=1, source_target_pairs={{16,0},{32,16},{48,32},{64,48},{80,64},{96,80},{112,96},{128,112},... | collective-permute-start | bytes 147464 | tf_op jit(solution)/shard_map/ppermute | solution.py:33
  43.0 2.0 %collective-permute-done.5 = bf16[2,2,3,1,1,512]{5,4,2,3,1,0:T(2,128)(2,1)S(1)} collective-permute-done((bf16[2,2,3,1,1,512]{5,4,2,3,1,0:T(2,128)(2,1)S(1)}, bf16[2,2,3,1,1,512]{5,4,2,3,1,0:T(2,128)(2,1)S(1)}, u32[]{:S(2)}, u32[]{:S(2)}) %collective-permute-start.5) | collective-permute-done | bytes 12320 | tf_op jit(solution)/shard_map/ppermute | solution.py:33
  45.6 1.6 %collective-permute-done.7 = bf16[2,2,3,1,4,512]{5,4,2,1,3,0:T(4,128)(2,1)S(1)} collective-permute-done((bf16[2,2,3,1,4,512]{5,4,2,1,3,0:T(4,128)(2,1)S(1)}, bf16[2,2,3,1,4,512]{5,4,2,1,3,0:T(4,128)(2,1)S(1)}, u32[]{:S(2)}, u32[]{:S(2)}) %collective-permute-start.7) | collective-permute-done | bytes 49184 | tf_op jit(solution)/shard_map/ppermute | solution.py:33
  47.3 0.3 bitcast_convert_fusion
  47.7 1.9 %multiply_reduce_fusion.1 = f32[4,512,24]{1,0,2:T(4,128)} fusion(f32[4,512,3,2,4]{1,0,2,4,3:T(4,128)S(1)} %bitcast_convert_fusion, bf16[24,2,4,3,1,4,512]{6,5,4,3,2,1,0:T(4,128)(2,1)S(1)} %copy-done.1), kind=kLoop, calls=%fused_computation.1 | loop fusion | flops 3489792 | bytes 2752512
  49.6 1.3 %copy.307 = f32[4,512,24]{2,1,0:T(8,128)S(1)} copy(f32[4,512,24]{1,0,2:T(4,128)} %multiply_reduce_fusion.1) | data formatting | bytes 393216 | tf_op jit(solution)/shard_map/vrsctzn,rsctzn->vtzn/dot_general | solution.py:149
  50.9 1.8 %fusion.1 = f32[32,24]{1,0:T(8,128)} fusion(f32[24,2048]{0,1:T(8,128)S(1)} %bitcast.1345, s32[2048]{0:T(1024)} %bitcast.1349), kind=kOutput, calls=%fused_computation.10 | convolution fusion | flops 18939904 | bytes 207872 | tf_op jit(solution)/shard_map/am,vm->av/dot_general | solution.py:155
  52.7 0.8 reshape.6851
  53.5 12.0 %psum.28 = f32[768]{0:T(1024)S(1)} all-reduce(f32[768]{0:T(1024)S(1)} %reshape.6851), channel_id=1, replica_groups=mesh['ta'=64,'gy'=4,'gx'=4] {'gx'}, use_global_device_ids=true, to_apply=%region_0.1 | all-reduce | flops 768 | bytes 6144 | tf_op jit(solution)/shard_map/psum | solution.py:158
  65.5 12.2 %psum.29 = f32[768]{0:T(1024)S(1)} all-reduce(f32[768]{0:T(1024)S(1)} %psum.28), channel_id=1, replica_groups=mesh['ta'=64,'gy'=4,'gx'=4] {'gy'}, use_global_device_ids=true, to_apply=%region_1.2 | all-reduce | flops 768 | bytes 6144 | tf_op jit(solution)/shard_map/psum | solution.py:158
  77.8 0.2 fusion
  78.0 0.3 dynamic_update_slice.3
  78.2 9.1 %psum.30 = bf16[768]{0:T(1024)(128)(2,1)S(1)} all-reduce(bf16[768]{0:T(1024)(128)(2,1)S(1)} %dynamic_update_slice.3), channel_id=1, replica_groups=mesh['ta'=64,'gy'=4,'gx'=4] {'gx'}, use_global_device_ids=true, to_apply=%region_2.3 | all-reduce | flops 768 | bytes 3072 | tf_op jit(solution)/shard_map/psum | solution.py:165
  87.3 0.1 reshape.6852
  87.4 11.1 %psum.31 = bf16[32,24]{1,0:T(8,128)(2,1)S(1)} all-reduce(bf16[32,24]{1,0:T(8,128)(2,1)S(1)} %reshape.6852), channel_id=1, replica_groups=mesh['ta'=64,'gy'=4,'gx'=4] {'gy'}, use_global_device_ids=true, to_apply=%region_3.4 | all-reduce | flops 768 | bytes 3072 | tf_op jit(solution)/shard_map/psum | solution.py:165
  98.5 0.9 convolution_convert_fusion
  99.4 1.3 %multiply_reduce_fusion = f32[4,512,2,4,3]{1,0,4,3,2:T(4,128)S(1)} fusion(f32[4,512,24]{1,0,2:T(4,128)S(1)} %bitcast_convert_fusion.2, bf16[24,2,4,3,1,4,512]{6,5,4,3,2,1,0:T(4,128)(2,1)S(1)} %copy-done.1), kind=kLoop, calls=%fused_computation | loop fusion | flops 3489792 | bytes 2752512 | tf_op jit(solution)/shard_map/vrsctzn,vtzn->rsctzn/dot_general | solution.py:172
  100.8 0.7 bitcast_add_fusion
  (271 shorter events, 5.5 us)
Async XLA Ops:
  0.0 77.8 %copy-start = (f32[1,48,768]{2,1,0:T(8,128)S(1)}, f32[1,48,768]{2,1,0:T(8,128)}, u32[]{:S(2)}) copy-start(f32[1,48,768]{2,1,0:T(8,128)} %param.11) | copy-start | bytes 442372
  2.1 27.0 %collective-permute-start = (bf16[2,2,3,1,1,512]{5,4,2,1,3,0:T(2,128)(2,1)S(1)}, bf16[2,2,3,1,1,512]{5,4,2,1,3,0:T(2,128)(2,1)S(1)}, u32[]{:S(2)}, u32[]{:S(2)}) collective-permute-start(bf16[2,2,3,1,1,512]{5,4,2,1,3,0:T(2,128)(2,1)S(1)} %pad_maximum_fusion.33), channel_id=1, source_target_pairs={{1,0},{2,1},{3,2},{4,3},{5,4},{6,5},{7,6},{8,7},{9,8},{10,9},{11,1... | collective-permute-start | bytes 36872 | tf_op jit(solution)/shard_map/ppermute | solution.py:33
  6.0 23.4 %collective-permute-start.1 = (bf16[2,2,3,1,1,512]{5,4,2,1,3,0:T(2,128)(2,1)S(1)}, bf16[2,2,3,1,1,512]{5,4,2,1,3,0:T(2,128)(2,1)S(1)}, u32[]{:S(2)}, u32[]{:S(2)}) collective-permute-start(bf16[2,2,3,1,1,512]{5,4,2,1,3,0:T(2,128)(2,1)S(1)} %fusion.65), channel_id=1, source_target_pairs={{15,0},{0,1},{1,2},{2,3},{3,4},{4,5},{5,6},{6,7},{7,8},{8,9},{9,10... | collective-permute-start | bytes 36872 | tf_op jit(solution)/shard_map/ppermute | solution.py:33
  9.5 20.2 %collective-permute-start.2 = (bf16[2,2,3,1,4,512]{5,4,2,1,3,0:T(4,128)(2,1)S(1)}, bf16[2,2,3,1,4,512]{5,4,2,1,3,0:T(4,128)(2,1)S(1)}, u32[]{:S(2)}, u32[]{:S(2)}) collective-permute-start(bf16[2,2,3,1,4,512]{5,4,2,1,3,0:T(4,128)(2,1)S(1)} %pad_maximum_fusion.21), channel_id=1, source_target_pairs={{16,0},{32,16},{48,32},{64,48},{80,64},{96,80},{112,96},{128,112},... | collective-permute-start | bytes 147464 | tf_op jit(solution)/shard_map/ppermute | solution.py:33
  25.6 4.7 %collective-permute-start.3 = (bf16[2,2,3,1,4,512]{5,4,2,3,1,0:T(4,128)(2,1)S(1)}, bf16[2,2,3,1,4,512]{5,4,2,3,1,0:T(4,128)(2,1)S(1)}, u32[]{:S(2)}, u32[]{:S(2)}) collective-permute-start(bf16[2,2,3,1,4,512]{5,4,2,3,1,0:T(4,128)(2,1)S(1)} %pad_maximum_fusion.23), channel_id=1, source_target_pairs={{1008,0},{0,16},{16,32},{32,48},{48,64},{64,80},{80,96},{96,112},{... | collective-permute-start | bytes 147464 | tf_op jit(solution)/shard_map/ppermute | solution.py:33
  27.5 1.0 %copy-start.5 = (s32[1,4,512]{2,1,0:T(4,128)S(1)}, s32[1,4,512]{2,1,0:T(4,128)}, u32[]{:S(2)}) copy-start(s32[1,4,512]{2,1,0:T(4,128)} %param.9) | copy-start | bytes 24580
  29.3 1.2 %copy-start.4 = (bf16[2,4,3,1,4,512]{5,4,3,2,1,0:T(4,128)(2,1)S(1)}, bf16[2,4,3,1,4,512]{5,4,3,2,1,0:T(4,128)(2,1)}, u32[]{:S(2)}) copy-start(bf16[2,4,3,1,4,512]{5,4,3,2,1,0:T(4,128)(2,1)} %param.6) | copy-start | bytes 294916
  30.9 16.4 %copy-start.2 = (f32[2,4,3,1,4,512]{5,4,3,2,1,0:T(4,128)}, f32[2,4,3,1,4,512]{5,4,3,2,1,0:T(4,128)S(1)}, u32[]{:S(2)}) copy-start(f32[2,4,3,1,4,512]{5,4,3,2,1,0:T(4,128)S(1)} %get-tuple-element.7) | copy-start | bytes 589828
  33.9 8.8 %collective-permute-start.4 = (bf16[2,2,3,1,1,512]{5,4,2,1,3,0:T(2,128)(2,1)S(1)}, bf16[2,2,3,1,1,512]{5,4,2,1,3,0:T(2,128)(2,1)S(1)}, u32[]{:S(2)}, u32[]{:S(2)}) collective-permute-start(bf16[2,2,3,1,1,512]{5,4,2,1,3,0:T(2,128)(2,1)S(1)} %pad_maximum_fusion.31), channel_id=1, source_target_pairs={{1,0},{2,1},{3,2},{4,3},{5,4},{6,5},{7,6},{8,7},{9,8},{10,9},{11,1... | collective-permute-start | bytes 36872 | tf_op jit(solution)/shard_map/ppermute | solution.py:33
  37.5 7.5 %collective-permute-start.5 = (bf16[2,2,3,1,1,512]{5,4,2,3,1,0:T(2,128)(2,1)S(1)}, bf16[2,2,3,1,1,512]{5,4,2,3,1,0:T(2,128)(2,1)S(1)}, u32[]{:S(2)}, u32[]{:S(2)}) collective-permute-start(bf16[2,2,3,1,1,512]{5,4,2,3,1,0:T(2,128)(2,1)S(1)} %fusion.61), channel_id=1, source_target_pairs={{15,0},{0,1},{1,2},{2,3},{3,4},{4,5},{5,6},{6,7},{7,8},{8,9},{9,10... | collective-permute-start | bytes 36872 | tf_op jit(solution)/shard_map/ppermute | solution.py:33
  40.1 5.2 %collective-permute-start.6 = (bf16[2,2,3,1,4,512]{5,4,2,1,3,0:T(4,128)(2,1)S(1)}, bf16[2,2,3,1,4,512]{5,4,2,1,3,0:T(4,128)(2,1)S(1)}, u32[]{:S(2)}, u32[]{:S(2)}) collective-permute-start(bf16[2,2,3,1,4,512]{5,4,2,1,3,0:T(4,128)(2,1)S(1)} %pad_maximum_fusion.28), channel_id=1, source_target_pairs={{16,0},{32,16},{48,32},{64,48},{80,64},{96,80},{112,96},{128,112},... | collective-permute-start | bytes 147464 | tf_op jit(solution)/shard_map/ppermute | solution.py:33
  42.4 4.7 %collective-permute-start.7 = (bf16[2,2,3,1,4,512]{5,4,2,1,3,0:T(4,128)(2,1)S(1)}, bf16[2,2,3,1,4,512]{5,4,2,1,3,0:T(4,128)(2,1)S(1)}, u32[]{:S(2)}, u32[]{:S(2)}) collective-permute-start(bf16[2,2,3,1,4,512]{5,4,2,1,3,0:T(4,128)(2,1)S(1)} %pad_maximum_fusion.29), channel_id=1, source_target_pairs={{1008,0},{0,16},{16,32},{32,48},{48,64},{64,80},{80,96},{96,112},{... | collective-permute-start | bytes 147464 | tf_op jit(solution)/shard_map/ppermute | solution.py:33
  45.2 2.4 %copy-start.1 = (bf16[24,2,4,3,1,4,512]{6,5,4,3,2,1,0:T(4,128)(2,1)S(1)}, bf16[24,2,4,3,1,4,512]{6,5,4,3,2,1,0:T(4,128)(2,1)}, u32[]{:S(2)}) copy-start(bf16[24,2,4,3,1,4,512]{6,5,4,3,2,1,0:T(4,128)(2,1)} %param.10) | copy-start | bytes 7077892
  52.7 48.1 %copy-start.3 = (f32[2,4,3,1,4,512]{5,4,3,2,1,0:T(4,128)S(1)}, f32[2,4,3,1,4,512]{5,4,3,2,1,0:T(4,128)}, u32[]{:S(2)}) copy-start(f32[2,4,3,1,4,512]{5,4,3,2,1,0:T(4,128)} %copy-done.2) | copy-start | bytes 589828

commit v3 on v2

--- a/solution.py
+++ b/solution.py
@@ -1,6 +1,8 @@
 import jax
 import jax.numpy as jnp
 from jax import lax
+from jax.experimental import pallas as pl
+from jax.experimental.pallas import tpu as pltpu
 from jax.sharding import Mesh, PartitionSpec as P
 
 LX = 32
@@ -28,7 +30,10 @@
 
 
 def shifted(block, axis, distance):
-    devices = range(16 if axis == GZ else lax.axis_size(axis))
+    count = 1
+    for name in axis if isinstance(axis, tuple) else (axis,):
+        count *= lax.axis_size(name)
+    devices = range(count)
     route = [((i - distance) % len(devices), i) for i in devices]
     return lax.ppermute(block, axis, route)
 
@@ -116,23 +121,159 @@
     return jnp.concatenate([shifted(edge, axis, 1), inner], axis=dim)
 
 
+def nested_project(wide, direction, sign):
+    rows = [[], []]
+    for slot in range(2):
+        other = spin_perms[direction][slot]
+        row_re, row_im = [], []
+        for color in range(3):
+            term_re, term_im = phase_mul(
+                spin_real[direction][slot],
+                spin_imag[direction][slot],
+                wide[0][other][color],
+                wide[1][other][color],
+            )
+            row_re.append(wide[0][slot][color] + sign * term_re)
+            row_im.append(wide[1][slot][color] + sign * term_im)
+        rows[0].append(row_re)
+        rows[1].append(row_im)
+    return rows
+
+
+def nested_expand(half, direction, sign):
+    rows = [[None] * 4, [None] * 4]
+    for slot in range(2):
+        other = spin_perms[direction][slot]
+        rows[0][slot] = half[0][slot]
+        rows[1][slot] = half[1][slot]
+        pairs = [
+            phase_mul(
+                spin_real[direction][other],
+                spin_imag[direction][other],
+                half[0][slot][color],
+                half[1][slot][color],
+            )
+            for color in range(3)
+        ]
+        rows[0][other] = [sign * pair[0] for pair in pairs]
+        rows[1][other] = [sign * pair[1] for pair in pairs]
+    return rows
+
+
+def nested_mix(link, spinor, dagger):
+    out = [[], []]
+    for spin in range(len(spinor[0])):
+        out_re, out_im = [], []
+        for row in range(3):
+            acc_re = None
+            acc_im = None
+            for col in range(3):
+                if dagger:
+                    entry_re = link[0][col][row]
+                    entry_im = -link[1][col][row]
+                else:
+                    entry_re = link[0][row][col]
+                    entry_im = link[1][row][col]
+                spin_re = spinor[0][spin][col]
+                spin_im = spinor[1][spin][col]
+                part_re = entry_re * spin_re - entry_im * spin_im
+                part_im = entry_re * spin_im + entry_im * spin_re
+                acc_re = part_re if acc_re is None else acc_re + part_re
+                acc_im = part_im if acc_im is None else acc_im + part_im
+            out_re.append(acc_re)
+            out_im.append(acc_im)
+        out[0].append(out_re)
+        out[1].append(out_im)
+    return out
+
+
+def nested_map(nested, fn):
+    return [[[fn(value) for value in colors] for colors in spins] for spins in nested]
+
+
+def nested_read(ref, spins):
+    return [
+        [[ref[(part * spins + spin) * 3 + color].astype(jnp.float32) for color in range(3)] for spin in range(spins)]
+        for part in range(2)
+    ]
+
+
+def hop_kernel(v_ref, u_ref, az_ref, bz_ref, at_ref, bt_ref, out_ref):
+    width = v_ref.shape[-1]
+    wide = nested_read(v_ref, 4)
+    column = lax.broadcasted_iota(jnp.int32, wide[0][0][0].shape, 1) % LX
+
+    def link(mu):
+        return [
+            [[u_ref[mu, (part * 3 + row) * 3 + col].astype(jnp.float32) for col in range(3)] for row in range(3)]
+            for part in range(2)
+        ]
+
+    def round_half(value):
+        return value.astype(jnp.bfloat16).astype(jnp.float32)
+
+    shifts_ahead = (
+        lambda a: jnp.where(column == LX - 1, pltpu.roll(a, LX - 1, 1), pltpu.roll(a, width - 1, 1)),
+        lambda a: pltpu.roll(a, width - LX, 1),
+    )
+    shifts_behind = (
+        lambda a: jnp.where(column == 0, pltpu.roll(a, width - LX + 1, 1), pltpu.roll(a, 1, 1)),
+        lambda a: pltpu.roll(a, LX, 1),
+    )
+    total = [[[None] * 3 for _ in range(4)] for _ in range(2)]
+
+    def accumulate(term):
+        for part in range(2):
+            for spin in range(4):
+                for color in range(3):
+                    value = term[part][spin][color]
+                    old = total[part][spin][color]
+                    total[part][spin][color] = value if old is None else old + value
+
+    for mu in range(4):
+        links = link(mu)
+        if mu < 2:
+            ahead = nested_map(nested_project(wide, mu, -1.0), lambda a: shifts_ahead[mu](round_half(a)))
+            back = nested_project(nested_mix(links, wide, True), mu, 1.0)
+            behind = nested_map(back, lambda a: shifts_behind[mu](round_half(a)))
+        else:
+            ahead = nested_read(az_ref if mu == 2 else at_ref, 2)
+            behind = nested_read(bz_ref if mu == 2 else bt_ref, 2)
+        accumulate(nested_expand(nested_mix(links, ahead, False), mu, -1.0))
+        accumulate(nested_expand(behind, mu, 1.0))
+    for part in range(2):
+        for spin in range(4):
+            for color in range(3):
+                out_ref[(part * 4 + spin) * 3 + color] = total[part][spin][color]
+
+
 def hopping(spinor, gauge_links):
     wide = spinor.astype(jnp.float32)
-    fwd = [project(wide, mu, -1.0).astype(jnp.bfloat16) for mu in range(4)]
-    back = [
-        project(color_mix(gauge_links[mu], spinor, True), mu, 1.0).astype(jnp.bfloat16)
-        for mu in range(4)
+    fwd_z = project(wide, 2, -1.0).astype(jnp.bfloat16)
+    fwd_t = project(wide, 3, -1.0).astype(jnp.bfloat16)
+    back_z = project(color_mix(gauge_links[2], spinor, True), 2, 1.0).astype(jnp.bfloat16)
+    back_t = project(color_mix(gauge_links[3], spinor, True), 3, 1.0).astype(jnp.bfloat16)
+    halves = [
+        halo(fwd_z, GZ, 4, 1),
+        halo(back_z, GZ, 4, -1),
+        halo(fwd_t, "ta", 3, 1),
+        halo(back_t, "ta", 3, -1),
     ]
-    ahead = [local_shift(fwd[0], 0, 1), local_shift(fwd[1], 1, 1)]
-    behind = [local_shift(back[0], 0, -1), local_shift(back[1], 1, -1)]
-    ahead += [halo(fwd[2], GZ, 4, 1), halo(fwd[3], "ta", 3, 1)]
-    behind += [halo(back[2], GZ, 4, -1), halo(back[3], "ta", 3, -1)]
-    total = None
-    for mu in range(4):
-        term = expand(color_mix(gauge_links[mu], ahead[mu], False), mu, -1.0)
-        term = term + expand(behind[mu].astype(jnp.float32), mu, 1.0)
-        total = term if total is None else total + term
-    return total
+    shape = spinor.shape
+    rows = shape[3] * shape[4]
+    width = shape[5]
+    flat = [half.reshape(12, rows, width) for half in halves]
+    links = gauge_links.reshape(4, 18, rows, width)
+    total = pl.pallas_call(
+        hop_kernel,
+        out_shape=jax.ShapeDtypeStruct((24, rows, width), jnp.float32),
+        in_specs=[pl.BlockSpec(memory_space=pltpu.VMEM)] * 6,
+        out_specs=pl.BlockSpec(memory_space=pltpu.VMEM),
+        cost_estimate=pl.CostEstimate(
+            flops=24 * 1024 * rows * width // 8, bytes_accessed=2 * 160 * rows * width, transcendentals=0
+        ),
+    )(spinor.reshape(24, rows, width), links, *flat)
+    return total.reshape(shape)
 
 
 def shards(source, gauge_links, clover_diag, agg_map, prolong, coarse_inverse):
@@ -158,9 +299,9 @@
     coarse_resid = lax.psum(lax.psum(partial_sum.reshape(-1), "gx"), "gy")
     own_rows = jnp.dot(coarse_inverse[0], coarse_resid, precision=highest)
     rows = own_rows.shape[0]
-    place = (lax.axis_index("gy") * 4 + lax.axis_index("gx")) * rows
+    place = (lax.axis_index("gy") * lax.axis_size("gx") + lax.axis_index("gx")) * rows
     padded = lax.dynamic_update_slice(
-        jnp.zeros((rows * 16,), jnp.bfloat16), own_rows.astype(jnp.bfloat16), (place,)
+        jnp.zeros((rows * lax.axis_size("gy") * lax.axis_size("gx"),), jnp.bfloat16), own_rows.astype(jnp.bfloat16), (place,)
     )
     correction_half = lax.psum(lax.psum(padded, "gx"), "gy").reshape(NAGG, vectors)
     spread = jnp.einsum(

time: 102 us -> 103 us (level)
  Pallas kernels: 0 us -> 4.54 us
  waiting for transfers between devices: 3.96 us -> 1.7 us
  starting transfers between devices: 29.4 us -> 31 us
  other arithmetic: 15.2 us -> 13.6 us
  between operations: 2.18 us -> 0.73 us
  blocking collectives: 44.4 us -> 43.2 us
    pallas_call x0 -> x2, Pallas kernels: none -> 4.54 us  [hopping(): pl.pallas_call(hop_kernel, out_shape=jax.ShapeDtypeStruct((24, rows, widt...]
    psum x2, blocking collectives: 24.3 us -> 21.5 us  [shards(): coarse_resid = lax.psum(lax.psum(partial_sum.reshape(-1), 'gx'), 'gy')]
    concatenate x2 -> x4, other arithmetic: 0.17 us -> 2.69 us  [the longest x2 1.35 us: halo(): return jnp.concatenate([shifted(edge, axis, 1), inner], axis=dim)]
    ppermute x8, waiting for transfers between devices: 3.96 us -> 1.7 us  [shifted(): return lax.ppermute(block, axis, route)]
    mul x31 -> x2, other arithmetic: 0.23 us -> 1.94 us  [the longest x1 0.97 us: shards(): 0.5 * hopping(first_half, gauge_links)]
    psum x1, blocking collectives: 9.07 us -> 10.7 us  [shards(): lax.psum(padded, 'gx')]
    ppermute x8, starting transfers between devices: 29.4 us -> 31 us  [shifted(): return lax.ppermute(block, axis, route)]
    another operation x52 -> x24, other arithmetic: 2.18 us -> 0.77 us  [project(): return jnp.stack([jnp.stack(rows_re), jnp.stack(rows_im)])]
  transfers between devices with their start and end apart: 8 -> 8, of which waited for: 3 -> 1; matrix products, arithmetic and copies ran while one was open for 7% -> 4% of each run, Pallas kernels for 0% -> 0%
where the time goes in v3:
time: 103 us; the launch traced here: 102 us
  blocking collectives  43.2 us (42%)
  starting transfers between devices  31 us (30%)
  other arithmetic  13.6 us (13%)
  Pallas kernels  4.54 us (4%)
  local copies, waits for them, and re-layouts  4.41 us (4%)
  matrix products  2.87 us (3%)
  waiting for transfers between devices  1.7 us (2%)
    ppermute x8, starting transfers between devices, shifted(): return lax.ppermute(block, axis, route)  31 us
    psum x2, blocking collectives, shards(): coarse_resid = lax.psum(lax.psum(partial_sum.reshape(-1), 'gx'), 'gy')  21.5 us
    psum x1, blocking collectives, shards(): lax.psum(lax.psum(padded, 'gx'), 'gy').reshape(NAGG, vectors)  11.1 us
    psum x1, blocking collectives, shards(): lax.psum(padded, 'gx')  10.7 us
    pallas_call x2, Pallas kernels, hopping(): pl.pallas_call(hop_kernel, out_shape=jax.ShapeDtypeStruct((24, rows, widt...  4.54 us
  transfers between devices with their start and end apart: 8, of which 1 were waited for; matrix products, arithmetic and copies ran while one was open for 4% of the time, Pallas kernels for 0%

profile of v3, /device:TPU:10, one launch (start us, length us, event | category | flops | bytes accessed | tf_op | source)
XLA Modules:
  0.0 102.0 jit_solution(15144400869007475369)
XLA Ops:
  0.0 0.9 bitcast_convert_fusion.3
  0.9 0.9 add_bitcast_fusion
  1.8 1.0 fusion.100
  2.8 0.1 subtract_add_fusion.8
  2.9 0.0 copy-start.11
  2.9 0.1 subtract_add_fusion.7
  3.0 0.1 subtract_add_fusion.6
  3.2 0.0 copy-start.5
  3.3 0.0 collective-permute-start.3
  3.4 0.1 add_add_fusion.11
  3.4 0.1 add_add_fusion.10
  3.5 0.1 add_add_fusion.9
  3.7 0.1 fusion.25
  3.8 3.4 %collective-permute-start.1 = (bf16[2,2,3,1,1,512]{5,4,2,1,3,0:T(2,128)(2,1)S(1)}, bf16[2,2,3,1,1,512]{5,4,2,1,3,0:T(2,128)(2,1)S(1)}, u32[]{:S(2)}, u32[]{:S(2)}) collective-permute-start(bf16[2,2,3,1,1,512]{5,4,2,1,3,0:T(2,128)(2,1)S(1)} %fusion.25), channel_id=1, source_target_pairs={{15,0},{0,1},{1,2},{2,3},{3,4},{4,5},{5,6},{6,7},{7,8},{8,9},{9,10... | collective-permute-start | bytes 36872 | tf_op jit(solution)/shard_map/ppermute | solution.py:38
  7.3 2.4 %collective-permute-start = (bf16[2,2,3,1,1,512]{5,4,2,1,3,0:T(2,128)(2,1)S(1)}, bf16[2,2,3,1,1,512]{5,4,2,1,3,0:T(2,128)(2,1)S(1)}, u32[]{:S(2)}, u32[]{:S(2)}) collective-permute-start(bf16[2,2,3,1,1,512]{5,4,2,1,3,0:T(2,128)(2,1)S(1)} %pad_maximum_fusion.12), channel_id=1, source_target_pairs={{1,0},{2,1},{3,2},{4,3},{5,4},{6,5},{7,6},{8,7},{9,8},{10,9},{11,1... | collective-permute-start | bytes 36872 | tf_op jit(solution)/shard_map/ppermute | solution.py:38
  9.9 15.7 %collective-permute-start.2 = (bf16[2,2,3,1,4,512]{5,4,2,1,3,0:T(4,128)(2,1)S(1)}, bf16[2,2,3,1,4,512]{5,4,2,1,3,0:T(4,128)(2,1)S(1)}, u32[]{:S(2)}, u32[]{:S(2)}) collective-permute-start(bf16[2,2,3,1,4,512]{5,4,2,1,3,0:T(4,128)(2,1)S(1)} %pad_maximum_fusion.6), channel_id=1, source_target_pairs={{16,0},{32,16},{48,32},{64,48},{80,64},{96,80},{112,96},{128,112},... | collective-permute-start | bytes 147464 | tf_op jit(solution)/shard_map/ppermute | solution.py:38
  25.5 0.1 slice_maximum_fusion.1
  25.6 0.6 copy.98
  26.2 0.0 collective-permute-done.1
  26.2 0.7 fusion.15
  26.9 0.0 collective-permute-done
  26.9 0.7 pad_maximum_fusion.5
  27.6 0.6 copy-done.7
  28.2 0.0 copy-done.9
  28.2 2.3 %shard_map.64 = f32[24,4,512]{2,1,0:T(4,128)} custom-call(bf16[24,4,512]{2,1,0:T(4,128)(2,1)} %bitcast.464, bf16[4,18,4,512]{3,2,1,0:T(4,128)(2,1)} %bitcast.460, bf16[12,4,512]{2,1,0:T(4,128)(2,1)} %bitcast.469, bf16[12,4,512]{2,1,0:T(4,128)(2,1)} %bitcast.467, bf16[12,4,512]{2,1,0:T(4,128)(2,1)} %bitcast.475, bf16[12,4,512]{2,1,0:T(4,128)(2,1)} %bitcast.473), custom_call_target="tpu_custom_call" | custom-call | flops 6291456 | bytes 655360 | tf_op jit(solution)/shard_map/pallas_call | solution.py:267
  30.5 1.0 broadcast_multiply_fusion.1
  31.4 0.1 bitcast_convert_fusion
  31.6 0.0 copy-start.2
  31.7 0.1 subtract_add_fusion.2
  31.7 0.1 subtract_add_fusion.1
  31.8 0.1 subtract_add_fusion
  31.9 0.1 add_add_fusion.5
  32.0 0.1 add_add_fusion.4
  32.0 0.0 copy-start.1
  32.1 0.1 add_add_fusion.3
  32.2 0.1 slice_maximum_fusion
  32.5 0.0 collective-permute-start.7
  32.7 0.1 fusion.24
  32.8 3.4 %collective-permute-start.5 = (bf16[2,2,3,1,1,512]{5,4,2,1,3,0:T(2,128)(2,1)S(1)}, bf16[2,2,3,1,1,512]{5,4,2,1,3,0:T(2,128)(2,1)S(1)}, u32[]{:S(2)}, u32[]{:S(2)}) collective-permute-start(bf16[2,2,3,1,1,512]{5,4,2,1,3,0:T(2,128)(2,1)S(1)} %fusion.24), channel_id=1, source_target_pairs={{15,0},{0,1},{1,2},{2,3},{3,4},{4,5},{5,6},{6,7},{7,8},{8,9},{9,10... | collective-permute-start | bytes 36872 | tf_op jit(solution)/shard_map/ppermute | solution.py:38
  36.3 2.7 %collective-permute-start.6 = (bf16[2,2,3,1,4,512]{5,4,2,1,3,0:T(4,128)(2,1)S(1)}, bf16[2,2,3,1,4,512]{5,4,2,1,3,0:T(4,128)(2,1)S(1)}, u32[]{:S(2)}, u32[]{:S(2)}) collective-permute-start(bf16[2,2,3,1,4,512]{5,4,2,1,3,0:T(4,128)(2,1)S(1)} %pad_maximum_fusion.9), channel_id=1, source_target_pairs={{16,0},{32,16},{48,32},{64,48},{80,64},{96,80},{112,96},{128,112},... | collective-permute-start | bytes 147464 | tf_op jit(solution)/shard_map/ppermute | solution.py:38
  39.0 3.3 %collective-permute-start.4 = (bf16[2,2,3,1,1,512]{5,4,2,1,3,0:T(2,128)(2,1)S(1)}, bf16[2,2,3,1,1,512]{5,4,2,1,3,0:T(2,128)(2,1)S(1)}, u32[]{:S(2)}, u32[]{:S(2)}) collective-permute-start(bf16[2,2,3,1,1,512]{5,4,2,1,3,0:T(2,128)(2,1)S(1)} %pad_maximum_fusion.11), channel_id=1, source_target_pairs={{1,0},{2,1},{3,2},{4,3},{5,4},{6,5},{7,6},{8,7},{9,8},{10,9},{11,1... | collective-permute-start | bytes 36872 | tf_op jit(solution)/shard_map/ppermute | solution.py:38
  42.3 0.7 fusion.12
  43.0 1.7 %collective-permute-done.4 = bf16[2,2,3,1,1,512]{5,4,2,1,3,0:T(2,128)(2,1)S(1)} collective-permute-done((bf16[2,2,3,1,1,512]{5,4,2,1,3,0:T(2,128)(2,1)S(1)}, bf16[2,2,3,1,1,512]{5,4,2,1,3,0:T(2,128)(2,1)S(1)}, u32[]{:S(2)}, u32[]{:S(2)}) %collective-permute-start.4) | collective-permute-done | bytes 12320 | tf_op jit(solution)/shard_map/ppermute | solution.py:38
  44.7 0.7 pad_maximum_fusion.8
  45.4 0.6 copy-done.8
  46.0 0.0 copy-done.10
  46.0 2.3 %shard_map.65 = f32[24,4,512]{2,1,0:T(4,128)} custom-call(bf16[24,4,512]{2,1,0:T(4,128)(2,1)} %bitcast.463, bf16[4,18,4,512]{3,2,1,0:T(4,128)(2,1)} %bitcast.461, bf16[12,4,512]{2,1,0:T(4,128)(2,1)} %bitcast.470, bf16[12,4,512]{2,1,0:T(4,128)(2,1)} %bitcast.468, bf16[12,4,512]{2,1,0:T(4,128)(2,1)} %bitcast.476, bf16[12,4,512]{2,1,0:T(4,128)(2,1)} %bitcast.474), custom_call_target="tpu_custom_call" | custom-call | flops 6291456 | bytes 655360 | tf_op jit(solution)/shard_map/pallas_call | solution.py:267
  48.3 1.0 broadcast_multiply_fusion
  49.2 0.1 fusion.10
  49.3 1.9 %multiply_reduce_fusion.1 = f32[4,512,24]{1,0,2:T(4,128)} fusion(f32[4,512,3,2,4]{1,0,2,4,3:T(4,128)S(1)} %fusion.10, bf16[24,2,4,3,1,4,512]{6,5,4,3,2,1,0:T(4,128)(2,1)S(1)} %copy-done.1), kind=kLoop, calls=%fused_computation.1 | loop fusion | flops 3489792 | bytes 2752512
  51.3 1.3 %copy.87 = f32[4,512,24]{2,1,0:T(8,128)S(1)} copy(f32[4,512,24]{1,0,2:T(4,128)} %multiply_reduce_fusion.1) | data formatting | bytes 393216 | tf_op jit(solution)/shard_map/vrsctzn,rsctzn->vtzn/dot_general | solution.py:290
  52.5 1.8 %fusion.1 = f32[32,24]{1,0:T(8,128)} fusion(f32[24,2048]{0,1:T(8,128)S(1)} %bitcast.459, s32[2048]{0:T(1024)} %bitcast.471), kind=kOutput, calls=%fused_computation.9 | convolution fusion | flops 18939904 | bytes 207872 | tf_op jit(solution)/shard_map/am,vm->av/dot_general | solution.py:296
  54.3 0.8 reshape.2121
  55.2 12.0 %psum.28 = f32[768]{0:T(1024)S(1)} all-reduce(f32[768]{0:T(1024)S(1)} %reshape.2121), channel_id=1, replica_groups=mesh['ta'=64,'gy'=4,'gx'=4] {'gx'}, use_global_device_ids=true, to_apply=%region_0.0 | all-reduce | flops 768 | bytes 6144 | tf_op jit(solution)/shard_map/psum | solution.py:299
  67.2 9.4 %psum.29 = f32[768]{0:T(1024)S(1)} all-reduce(f32[768]{0:T(1024)S(1)} %psum.28), channel_id=1, replica_groups=mesh['ta'=64,'gy'=4,'gx'=4] {'gy'}, use_global_device_ids=true, to_apply=%region_1.0 | all-reduce | flops 768 | bytes 6144 | tf_op jit(solution)/shard_map/psum | solution.py:299
  76.7 0.2 fusion
  76.8 0.3 dynamic_update_slice.3
  77.1 10.7 %psum.30 = bf16[768]{0:T(1024)(128)(2,1)S(1)} all-reduce(bf16[768]{0:T(1024)(128)(2,1)S(1)} %dynamic_update_slice.3), channel_id=1, replica_groups=mesh['ta'=64,'gy'=4,'gx'=4] {'gx'}, use_global_device_ids=true, to_apply=%region_2.0 | all-reduce | flops 768 | bytes 3072 | tf_op jit(solution)/shard_map/psum | solution.py:306
  87.8 0.1 reshape.2122
  87.9 11.1 %psum.31 = bf16[32,24]{1,0:T(8,128)(2,1)S(1)} all-reduce(bf16[32,24]{1,0:T(8,128)(2,1)S(1)} %reshape.2122), channel_id=1, replica_groups=mesh['ta'=64,'gy'=4,'gx'=4] {'gy'}, use_global_device_ids=true, to_apply=%region_3.0 | all-reduce | flops 768 | bytes 3072 | tf_op jit(solution)/shard_map/psum | solution.py:306
  99.0 0.9 convolution_convert_fusion
  99.8 0.1 reshape.2123
  99.9 1.3 %multiply_reduce_fusion = f32[4,512,2,4,3]{1,0,4,3,2:T(4,128)S(1)} fusion(f32[4,512,24]{1,0,2:T(4,128)S(1)} %bitcast_convert_fusion.1, bf16[24,2,4,3,1,4,512]{6,5,4,3,2,1,0:T(4,128)(2,1)S(1)} %copy-done.1), kind=kLoop, calls=%fused_computation | loop fusion | flops 3489792 | bytes 2752512 | tf_op jit(solution)/shard_map/vrsctzn,vtzn->rsctzn/dot_general | solution.py:313
  101.2 0.7 bitcast_add_fusion
  (70 shorter events, 1.2 us)
Async XLA Ops:
  0.0 76.7 %copy-start = (f32[1,48,768]{2,1,0:T(8,128)S(1)}, f32[1,48,768]{2,1,0:T(8,128)}, u32[]{:S(2)}) copy-start(f32[1,48,768]{2,1,0:T(8,128)} %param.11) | copy-start | bytes 442372
  2.8 1.0 copy-start.6
  2.9 22.7 %copy-start.11 = (s32[1,4,512]{2,1,0:T(4,128)S(1)}, s32[1,4,512]{2,1,0:T(4,128)}, u32[]{:S(2)}) copy-start(s32[1,4,512]{2,1,0:T(4,128)} %param.9) | copy-start | bytes 24580
  3.2 28.3 %copy-start.5 = (bf16[2,4,3,1,4,512]{5,4,3,2,1,0:T(4,128)(2,1)S(1)}, bf16[2,4,3,1,4,512]{5,4,3,2,1,0:T(4,128)(2,1)}, u32[]{:S(2)}) copy-start(bf16[2,4,3,1,4,512]{5,4,3,2,1,0:T(4,128)(2,1)} %param.6) | copy-start | bytes 294916
  3.3 24.3 %collective-permute-start.3 = (bf16[2,2,3,1,4,512]{5,4,2,1,3,0:T(4,128)(2,1)S(1)}, bf16[2,2,3,1,4,512]{5,4,2,1,3,0:T(4,128)(2,1)S(1)}, u32[]{:S(2)}, u32[]{:S(2)}) collective-permute-start(bf16[2,2,3,1,4,512]{5,4,2,1,3,0:T(4,128)(2,1)S(1)} %pad_maximum_fusion.7), channel_id=1, source_target_pairs={{1008,0},{0,16},{16,32},{32,48},{48,64},{64,80},{80,96},{96,112},{... | collective-permute-start | bytes 147464 | tf_op jit(solution)/shard_map/ppermute | solution.py:38
  3.8 22.4 %collective-permute-start.1 = (bf16[2,2,3,1,1,512]{5,4,2,1,3,0:T(2,128)(2,1)S(1)}, bf16[2,2,3,1,1,512]{5,4,2,1,3,0:T(2,128)(2,1)S(1)}, u32[]{:S(2)}, u32[]{:S(2)}) collective-permute-start(bf16[2,2,3,1,1,512]{5,4,2,1,3,0:T(2,128)(2,1)S(1)} %fusion.25), channel_id=1, source_target_pairs={{15,0},{0,1},{1,2},{2,3},{3,4},{4,5},{5,6},{6,7},{7,8},{8,9},{9,10... | collective-permute-start | bytes 36872 | tf_op jit(solution)/shard_map/ppermute | solution.py:38
  7.3 19.6 %collective-permute-start = (bf16[2,2,3,1,1,512]{5,4,2,1,3,0:T(2,128)(2,1)S(1)}, bf16[2,2,3,1,1,512]{5,4,2,1,3,0:T(2,128)(2,1)S(1)}, u32[]{:S(2)}, u32[]{:S(2)}) collective-permute-start(bf16[2,2,3,1,1,512]{5,4,2,1,3,0:T(2,128)(2,1)S(1)} %pad_maximum_fusion.12), channel_id=1, source_target_pairs={{1,0},{2,1},{3,2},{4,3},{5,4},{6,5},{7,6},{8,7},{9,8},{10,9},{11,1... | collective-permute-start | bytes 36872 | tf_op jit(solution)/shard_map/ppermute | solution.py:38
  9.9 17.7 %collective-permute-start.2 = (bf16[2,2,3,1,4,512]{5,4,2,1,3,0:T(4,128)(2,1)S(1)}, bf16[2,2,3,1,4,512]{5,4,2,1,3,0:T(4,128)(2,1)S(1)}, u32[]{:S(2)}, u32[]{:S(2)}) collective-permute-start(bf16[2,2,3,1,4,512]{5,4,2,1,3,0:T(4,128)(2,1)S(1)} %pad_maximum_fusion.6), channel_id=1, source_target_pairs={{16,0},{32,16},{48,32},{64,48},{80,64},{96,80},{112,96},{128,112},... | collective-permute-start | bytes 147464 | tf_op jit(solution)/shard_map/ppermute | solution.py:38
  27.6 0.6 copy-start.7
  27.6 0.6 copy-start.9
  31.6 4.6 %copy-start.4 = (bf16[2,4,3,1,4,512]{5,4,3,2,1,0:T(4,128)(2,1)}, bf16[2,4,3,1,4,512]{5,4,3,2,1,0:T(4,128)(2,1)S(1)}, u32[]{:S(2)}) copy-start(bf16[2,4,3,1,4,512]{5,4,3,2,1,0:T(4,128)(2,1)S(1)} %get-tuple-element.6) | copy-start | bytes 294916
  31.6 17.6 %copy-start.2 = (f32[2,4,3,1,4,512]{5,4,3,2,1,0:T(4,128)}, f32[2,4,3,1,4,512]{5,4,3,2,1,0:T(4,128)S(1)}, u32[]{:S(2)}) copy-start(f32[2,4,3,1,4,512]{5,4,3,2,1,0:T(4,128)S(1)} %get-tuple-element.7) | copy-start | bytes 589828
  32.0 17.3 %copy-start.1 = (bf16[24,2,4,3,1,4,512]{6,5,4,3,2,1,0:T(4,128)(2,1)S(1)}, bf16[24,2,4,3,1,4,512]{6,5,4,3,2,1,0:T(4,128)(2,1)}, u32[]{:S(2)}) copy-start(bf16[24,2,4,3,1,4,512]{6,5,4,3,2,1,0:T(4,128)(2,1)} %param.10) | copy-start | bytes 7077892
  32.5 12.8 %collective-permute-start.7 = (bf16[2,2,3,1,4,512]{5,4,2,1,3,0:T(4,128)(2,1)S(1)}, bf16[2,2,3,1,4,512]{5,4,2,1,3,0:T(4,128)(2,1)S(1)}, u32[]{:S(2)}, u32[]{:S(2)}) collective-permute-start(bf16[2,2,3,1,4,512]{5,4,2,1,3,0:T(4,128)(2,1)S(1)} %pad_maximum_fusion.10), channel_id=1, source_target_pairs={{1008,0},{0,16},{16,32},{32,48},{48,64},{64,80},{80,96},{96,112},{... | collective-permute-start | bytes 147464 | tf_op jit(solution)/shard_map/ppermute | solution.py:38
  32.8 9.5 %collective-permute-start.5 = (bf16[2,2,3,1,1,512]{5,4,2,1,3,0:T(2,128)(2,1)S(1)}, bf16[2,2,3,1,1,512]{5,4,2,1,3,0:T(2,128)(2,1)S(1)}, u32[]{:S(2)}, u32[]{:S(2)}) collective-permute-start(bf16[2,2,3,1,1,512]{5,4,2,1,3,0:T(2,128)(2,1)S(1)} %fusion.24), channel_id=1, source_target_pairs={{15,0},{0,1},{1,2},{2,3},{3,4},{4,5},{5,6},{6,7},{7,8},{8,9},{9,10... | collective-permute-start | bytes 36872 | tf_op jit(solution)/shard_map/ppermute | solution.py:38
  36.3 9.1 %collective-permute-start.6 = (bf16[2,2,3,1,4,512]{5,4,2,1,3,0:T(4,128)(2,1)S(1)}, bf16[2,2,3,1,4,512]{5,4,2,1,3,0:T(4,128)(2,1)S(1)}, u32[]{:S(2)}, u32[]{:S(2)}) collective-permute-start(bf16[2,2,3,1,4,512]{5,4,2,1,3,0:T(4,128)(2,1)S(1)} %pad_maximum_fusion.9), channel_id=1, source_target_pairs={{16,0},{32,16},{48,32},{64,48},{80,64},{96,80},{112,96},{128,112},... | collective-permute-start | bytes 147464 | tf_op jit(solution)/shard_map/ppermute | solution.py:38
  39.0 5.7 %collective-permute-start.4 = (bf16[2,2,3,1,1,512]{5,4,2,1,3,0:T(2,128)(2,1)S(1)}, bf16[2,2,3,1,1,512]{5,4,2,1,3,0:T(2,128)(2,1)S(1)}, u32[]{:S(2)}, u32[]{:S(2)}) collective-permute-start(bf16[2,2,3,1,1,512]{5,4,2,1,3,0:T(2,128)(2,1)S(1)} %pad_maximum_fusion.11), channel_id=1, source_target_pairs={{1,0},{2,1},{3,2},{4,3},{5,4},{6,5},{7,6},{8,7},{9,8},{10,9},{11,1... | collective-permute-start | bytes 36872 | tf_op jit(solution)/shard_map/ppermute | solution.py:38
  45.3 0.6 copy-start.8
  45.3 0.6 copy-start.10
  54.3 46.9 %copy-start.3 = (f32[2,4,3,1,4,512]{5,4,3,2,1,0:T(4,128)S(1)}, f32[2,4,3,1,4,512]{5,4,3,2,1,0:T(4,128)}, u32[]{:S(2)}) copy-start(f32[2,4,3,1,4,512]{5,4,3,2,1,0:T(4,128)} %copy-done.2) | copy-start | bytes 589828

commit v4 on v3

--- a/solution.py
+++ b/solution.py
@@ -292,10 +292,15 @@
     )
     vectors = prolong.shape[0]
     labels = jnp.arange(NAGG, dtype=jnp.int32)
-    member = agg_map.reshape(-1)[None, :] == labels[:, None]
-    partial_sum = jnp.einsum(
-        "am,vm->av", member.astype(jnp.float32), projected.reshape(vectors, -1), precision=highest
-    )
+    member = (agg_map[None] == labels[:, None, None, None]).astype(jnp.bfloat16)
+    high = projected.astype(jnp.bfloat16)
+    rest = projected - high.astype(jnp.float32)
+    middle = rest.astype(jnp.bfloat16)
+    low = (rest - middle.astype(jnp.float32)).astype(jnp.bfloat16)
+    partial_sum = None
+    for piece in (high, middle, low):
+        term = jnp.einsum("atzn,vtzn->av", member, piece, preferred_element_type=jnp.float32)
+        partial_sum = term if partial_sum is None else partial_sum + term
     coarse_resid = lax.psum(lax.psum(partial_sum.reshape(-1), "gx"), "gy")
     own_rows = jnp.dot(coarse_inverse[0], coarse_resid, precision=highest)
     rows = own_rows.shape[0]
@@ -305,16 +310,10 @@
     )
     correction_half = lax.psum(lax.psum(padded, "gx"), "gy").reshape(NAGG, vectors)
     spread = jnp.einsum(
-        "av,am->vm",
-        correction_half,
-        member.astype(jnp.bfloat16),
-        preferred_element_type=jnp.float32,
+        "av,atzn->vtzn", correction_half, member, preferred_element_type=jnp.float32
     ).astype(jnp.bfloat16)
     smooth = jnp.einsum(
-        "vrsctzn,vtzn->rsctzn",
-        prolong,
-        spread.reshape(projected.shape),
-        preferred_element_type=jnp.float32,
+        "vrsctzn,vtzn->rsctzn", prolong, spread, preferred_element_type=jnp.float32
     )
     return second_iter + smooth
 

time: 103 us -> 100 us (0.971)
  waiting for transfers between devices: 1.7 us -> 7.47 us
  starting transfers between devices: 31 us -> 28 us
  local copies, waits for them, and re-layouts: 4.41 us -> 1.79 us
  matrix products: 2.87 us -> 0.99 us
    ppermute x8, waiting for transfers between devices: 1.7 us -> 7.47 us  [shifted(): return lax.ppermute(block, axis, route)]
    psum x2, blocking collectives: 21.5 us -> 25 us  [shards(): coarse_resid = lax.psum(lax.psum(partial_sum.reshape(-1), 'gx'), 'gy')]
    psum x1, blocking collectives: 10.7 us -> 7.72 us  [shards(): lax.psum(padded, 'gx')]
    ppermute x8, starting transfers between devices: 31 us -> 28 us  [shifted(): return lax.ppermute(block, axis, route)]
    dot_general x2 -> x4, matrix products: 2.69 us -> 0.81 us  [the longest x3 0.61 us: shards(): jnp.einsum('atzn,vtzn->av', member, piece, preferred_element_type=jnp.flo...]
    dot_general x1 -> x0, local copies, waits for them, and re-layouts: 1.27 us -> none  [shards(): jnp.einsum('vrsctzn,rsctzn->vtzn', prolong, resid_half, preferred_element...]
  transfers between devices with their start and end apart: 8 -> 8, of which waited for: 1 -> 2; matrix products, arithmetic and copies ran while one was open for 4% -> 5% of each run, Pallas kernels for 0% -> 0%
where the time goes in v4:
time: 100 us; the launch traced here: 99.5 us
  blocking collectives  43.1 us (43%)
  starting transfers between devices  28 us (28%)
  other arithmetic  12.9 us (13%)
  waiting for transfers between devices  7.47 us (7%)
  Pallas kernels  4.55 us (5%)
  local copies, waits for them, and re-layouts  1.79 us (2%)
    ppermute x8, starting transfers between devices, shifted(): return lax.ppermute(block, axis, route)  28 us
    psum x2, blocking collectives, shards(): coarse_resid = lax.psum(lax.psum(partial_sum.reshape(-1), 'gx'), 'gy')  25 us
    psum x1, blocking collectives, shards(): lax.psum(lax.psum(padded, 'gx'), 'gy').reshape(NAGG, vectors)  10.4 us
    psum x1, blocking collectives, shards(): lax.psum(padded, 'gx')  7.72 us
    ppermute x8, waiting for transfers between devices, shifted(): return lax.ppermute(block, axis, route)  7.47 us
    pallas_call x2, Pallas kernels, hopping(): pl.pallas_call(hop_kernel, out_shape=jax.ShapeDtypeStruct((24, rows, widt...  4.55 us
  transfers between devices with their start and end apart: 8, of which 2 were waited for; matrix products, arithmetic and copies ran while one was open for 5% of the time, Pallas kernels for 0%

profile of v4, /device:TPU:10, one launch (start us, length us, event | category | flops | bytes accessed | tf_op | source)
XLA Modules:
  0.0 99.5 jit_solution(13368954019195642836)
XLA Ops:
  0.0 1.0 add_bitcast_fusion
  1.0 1.0 fusion.112
  2.1 2.4 %collective-permute-start = (bf16[2,2,3,1,1,512]{5,4,2,1,3,0:T(2,128)(2,1)S(1)}, bf16[2,2,3,1,1,512]{5,4,2,1,3,0:T(2,128)(2,1)S(1)}, u32[]{:S(2)}, u32[]{:S(2)}) collective-permute-start(bf16[2,2,3,1,1,512]{5,4,2,1,3,0:T(2,128)(2,1)S(1)} %pad_maximum_fusion.12), channel_id=1, source_target_pairs={{1,0},{2,1},{3,2},{4,3},{5,4},{6,5},{7,6},{8,7},{9,8},{10,9},{11,1... | collective-permute-start | bytes 36872 | tf_op jit(solution)/shard_map/ppermute | solution.py:38
  4.5 0.8 bitcast_convert_fusion.3
  5.4 0.1 add_add_fusion.9
  5.5 0.1 add_add_fusion.10
  5.6 0.1 add_add_fusion.11
  5.7 0.0 copy-start.3
  5.8 0.1 fusion.36
  5.9 3.4 %collective-permute-start.1 = (bf16[2,2,3,1,1,512]{5,4,2,1,3,0:T(2,128)(2,1)S(1)}, bf16[2,2,3,1,1,512]{5,4,2,1,3,0:T(2,128)(2,1)S(1)}, u32[]{:S(2)}, u32[]{:S(2)}) collective-permute-start(bf16[2,2,3,1,1,512]{5,4,2,1,3,0:T(2,128)(2,1)S(1)} %fusion.36), channel_id=1, source_target_pairs={{15,0},{0,1},{1,2},{2,3},{3,4},{4,5},{5,6},{6,7},{7,8},{8,9},{9,10... | collective-permute-start | bytes 36872 | tf_op jit(solution)/shard_map/ppermute | solution.py:38
  9.4 15.7 %collective-permute-start.2 = (bf16[2,2,3,1,4,512]{5,4,2,1,3,0:T(4,128)(2,1)S(1)}, bf16[2,2,3,1,4,512]{5,4,2,1,3,0:T(4,128)(2,1)S(1)}, u32[]{:S(2)}, u32[]{:S(2)}) collective-permute-start(bf16[2,2,3,1,4,512]{5,4,2,1,3,0:T(4,128)(2,1)S(1)} %pad_maximum_fusion.6), channel_id=1, source_target_pairs={{16,0},{32,16},{48,32},{64,48},{80,64},{96,80},{112,96},{128,112},... | collective-permute-start | bytes 147464 | tf_op jit(solution)/shard_map/ppermute | solution.py:38
  25.1 0.1 subtract_add_fusion.6
  25.1 0.1 subtract_add_fusion.7
  25.2 0.1 subtract_add_fusion.8
  25.5 0.0 collective-permute-start.3
  25.5 0.1 slice_maximum_fusion.1
  25.6 0.7 fusion.26
  26.3 0.0 collective-permute-done
  26.3 0.7 pad_maximum_fusion.5
  27.0 3.3 %collective-permute-done.3 = bf16[2,2,3,1,4,512]{5,4,2,1,3,0:T(4,128)(2,1)S(1)} collective-permute-done((bf16[2,2,3,1,4,512]{5,4,2,1,3,0:T(4,128)(2,1)S(1)}, bf16[2,2,3,1,4,512]{5,4,2,1,3,0:T(4,128)(2,1)S(1)}, u32[]{:S(2)}, u32[]{:S(2)}) %collective-permute-start.3) | collective-permute-done | bytes 49184 | tf_op jit(solution)/shard_map/ppermute | solution.py:38
  30.2 0.6 copy-done.7
  30.8 2.3 %shard_map.64 = f32[24,4,512]{2,1,0:T(4,128)} custom-call(bf16[24,4,512]{2,1,0:T(4,128)(2,1)} %bitcast.501, bf16[4,18,4,512]{3,2,1,0:T(4,128)(2,1)} %bitcast.497, bf16[12,4,512]{2,1,0:T(4,128)(2,1)} %bitcast.506, bf16[12,4,512]{2,1,0:T(4,128)(2,1)} %bitcast.504, bf16[12,4,512]{2,1,0:T(4,128)(2,1)} %bitcast.508, bf16[12,4,512]{2,1,0:T(4,128)(2,1)} %bitcast.510), custom_call_target="tpu_custom_call" | custom-call | flops 6291456 | bytes 655360 | tf_op jit(solution)/shard_map/pallas_call | solution.py:267
  33.1 1.0 broadcast_multiply_fusion.1
  34.1 0.1 bitcast_convert_fusion.1
  34.4 0.1 slice_maximum_fusion
  34.5 0.1 add_add_fusion.3
  34.6 0.1 add_add_fusion.4
  34.6 0.1 add_add_fusion.5
  34.7 0.1 subtract_add_fusion
  34.8 0.0 copy-start.1
  34.8 0.1 subtract_add_fusion.1
  34.8 0.1 subtract_add_fusion.2
  34.9 3.5 %collective-permute-start.4 = (bf16[2,2,3,1,1,512]{5,4,2,1,3,0:T(2,128)(2,1)S(1)}, bf16[2,2,3,1,1,512]{5,4,2,1,3,0:T(2,128)(2,1)S(1)}, u32[]{:S(2)}, u32[]{:S(2)}) collective-permute-start(bf16[2,2,3,1,1,512]{5,4,2,1,3,0:T(2,128)(2,1)S(1)} %pad_maximum_fusion.11), channel_id=1, source_target_pairs={{1,0},{2,1},{3,2},{4,3},{5,4},{6,5},{7,6},{8,7},{9,8},{10,9},{11,1... | collective-permute-start | bytes 36872 | tf_op jit(solution)/shard_map/ppermute | solution.py:38
  38.6 0.1 fusion.35
  38.6 2.5 %collective-permute-start.5 = (bf16[2,2,3,1,1,512]{5,4,2,1,3,0:T(2,128)(2,1)S(1)}, bf16[2,2,3,1,1,512]{5,4,2,1,3,0:T(2,128)(2,1)S(1)}, u32[]{:S(2)}, u32[]{:S(2)}) collective-permute-start(bf16[2,2,3,1,1,512]{5,4,2,1,3,0:T(2,128)(2,1)S(1)} %fusion.35), channel_id=1, source_target_pairs={{15,0},{0,1},{1,2},{2,3},{3,4},{4,5},{5,6},{6,7},{7,8},{8,9},{9,10... | collective-permute-start | bytes 36872 | tf_op jit(solution)/shard_map/ppermute | solution.py:38
  41.2 0.0 collective-permute-start.6
  41.5 0.5 collective-permute-start.7
  42.0 4.2 %collective-permute-done.5 = bf16[2,2,3,1,1,512]{5,4,2,1,3,0:T(2,128)(2,1)S(1)} collective-permute-done((bf16[2,2,3,1,1,512]{5,4,2,1,3,0:T(2,128)(2,1)S(1)}, bf16[2,2,3,1,1,512]{5,4,2,1,3,0:T(2,128)(2,1)S(1)}, u32[]{:S(2)}, u32[]{:S(2)}) %collective-permute-start.5) | collective-permute-done | bytes 12320 | tf_op jit(solution)/shard_map/ppermute | solution.py:38
  46.2 0.7 fusion.23
  46.9 0.7 pad_maximum_fusion.8
  47.5 0.0 collective-permute-done.6
  47.5 0.0 collective-permute-done.7
  47.5 0.6 copy-done.6
  48.1 0.0 copy-done.8
  48.2 2.3 %shard_map.65 = f32[24,4,512]{2,1,0:T(4,128)} custom-call(bf16[24,4,512]{2,1,0:T(4,128)(2,1)} %bitcast.500, bf16[4,18,4,512]{3,2,1,0:T(4,128)(2,1)} %bitcast.498, bf16[12,4,512]{2,1,0:T(4,128)(2,1)} %bitcast.507, bf16[12,4,512]{2,1,0:T(4,128)(2,1)} %bitcast.505, bf16[12,4,512]{2,1,0:T(4,128)(2,1)} %bitcast.509, bf16[12,4,512]{2,1,0:T(4,128)(2,1)} %bitcast.511), custom_call_target="tpu_custom_call" | custom-call | flops 6291456 | bytes 655360 | tf_op jit(solution)/shard_map/pallas_call | solution.py:267
  50.4 1.0 broadcast_multiply_fusion
  51.4 0.1 fusion.20
  51.5 1.3 %multiply_reduce_fusion.1 = f32[4,512,24]{1,0,2:T(4,128)S(1)} fusion(f32[4,512,3,2,4]{1,0,2,4,3:T(4,128)S(1)} %fusion.20, bf16[24,2,4,3,1,4,512]{6,5,4,3,2,1,0:T(4,128)(2,1)S(1)} %copy-done.1), kind=kLoop, calls=%fused_computation.1 | loop fusion | flops 3489792 | bytes 2752512
  52.8 0.2 convolution_bitcast_fusion
  53.0 0.2 convolution_bitcast_fusion.1
  53.2 0.2 fusion.1
  53.4 0.1 copy.79
  53.5 0.1 reshape.2136
  53.6 11.9 %psum.28 = f32[768]{0:T(1024)S(1)} all-reduce(f32[768]{0:T(1024)S(1)} %reshape.2136), channel_id=1, replica_groups=mesh['ta'=64,'gy'=4,'gx'=4] {'gx'}, use_global_device_ids=true, to_apply=%region_0.0 | all-reduce | flops 768 | bytes 6144 | tf_op jit(solution)/shard_map/psum | solution.py:304
  65.4 13.2 %psum.29 = f32[768]{0:T(1024)S(1)} all-reduce(f32[768]{0:T(1024)S(1)} %psum.28), channel_id=1, replica_groups=mesh['ta'=64,'gy'=4,'gx'=4] {'gy'}, use_global_device_ids=true, to_apply=%region_1.0 | all-reduce | flops 768 | bytes 6144 | tf_op jit(solution)/shard_map/psum | solution.py:304
  78.6 0.2 fusion.2
  78.8 0.3 dynamic_update_slice.3
  79.1 7.7 %psum.30 = bf16[768]{0:T(1024)(128)(2,1)S(1)} all-reduce(bf16[768]{0:T(1024)(128)(2,1)S(1)} %dynamic_update_slice.3), channel_id=1, replica_groups=mesh['ta'=64,'gy'=4,'gx'=4] {'gx'}, use_global_device_ids=true, to_apply=%region_2.0 | all-reduce | flops 768 | bytes 3072 | tf_op jit(solution)/shard_map/psum | solution.py:311
  86.8 0.1 reshape.2137
  86.9 10.4 %psum.31 = bf16[32,24]{1,0:T(8,128)(2,1)S(1)} all-reduce(bf16[32,24]{1,0:T(8,128)(2,1)S(1)} %reshape.2137), channel_id=1, replica_groups=mesh['ta'=64,'gy'=4,'gx'=4] {'gy'}, use_global_device_ids=true, to_apply=%region_3.0 | all-reduce | flops 768 | bytes 3072 | tf_op jit(solution)/shard_map/psum | solution.py:311
  97.2 0.2 convolution_convert_fusion
  97.4 0.1 fusion.21
  97.5 1.3 %multiply_reduce_fusion = f32[4,512,2,4,3]{1,0,4,3,2:T(4,128)S(1)} fusion(f32[4,512,24]{1,0,2:T(4,128)S(1)} %fusion.21, bf16[24,2,4,3,1,4,512]{6,5,4,3,2,1,0:T(4,128)(2,1)S(1)} %copy-done.1), kind=kLoop, calls=%fused_computation | loop fusion | flops 3489792 | bytes 2752512 | tf_op jit(solution)/shard_map/vrsctzn,vtzn->rsctzn/dot_general | solution.py:315
  98.8 0.7 bitcast_add_fusion
  (66 shorter events, 1.2 us)
Async XLA Ops:
  0.0 78.6 %copy-start = (f32[1,48,768]{2,1,0:T(8,128)S(1)}, f32[1,48,768]{2,1,0:T(8,128)}, u32[]{:S(2)}) copy-start(f32[1,48,768]{2,1,0:T(8,128)} %param.11) | copy-start | bytes 442372
  1.9 23.3 %copy-start.4 = (bf16[2,4,3,1,4,512]{5,4,2,3,1,0:T(4,128)(2,1)}, bf16[2,4,3,1,4,512]{5,4,2,3,1,0:T(4,128)(2,1)S(1)}, u32[]{:S(2)}) copy-start(bf16[2,4,3,1,4,512]{5,4,2,3,1,0:T(4,128)(2,1)S(1)} %get-tuple-element.9) | copy-start | bytes 294916
  2.1 24.2 %collective-permute-start = (bf16[2,2,3,1,1,512]{5,4,2,1,3,0:T(2,128)(2,1)S(1)}, bf16[2,2,3,1,1,512]{5,4,2,1,3,0:T(2,128)(2,1)S(1)}, u32[]{:S(2)}, u32[]{:S(2)}) collective-permute-start(bf16[2,2,3,1,1,512]{5,4,2,1,3,0:T(2,128)(2,1)S(1)} %pad_maximum_fusion.12), channel_id=1, source_target_pairs={{1,0},{2,1},{3,2},{4,3},{5,4},{6,5},{7,6},{8,7},{9,8},{10,9},{11,1... | collective-permute-start | bytes 36872 | tf_op jit(solution)/shard_map/ppermute | solution.py:38
  5.7 28.4 %copy-start.3 = (bf16[2,4,3,1,4,512]{5,4,3,2,1,0:T(4,128)(2,1)S(1)}, bf16[2,4,3,1,4,512]{5,4,3,2,1,0:T(4,128)(2,1)}, u32[]{:S(2)}) copy-start(bf16[2,4,3,1,4,512]{5,4,3,2,1,0:T(4,128)(2,1)} %param.6) | copy-start | bytes 294916
  5.9 19.7 %collective-permute-start.1 = (bf16[2,2,3,1,1,512]{5,4,2,1,3,0:T(2,128)(2,1)S(1)}, bf16[2,2,3,1,1,512]{5,4,2,1,3,0:T(2,128)(2,1)S(1)}, u32[]{:S(2)}, u32[]{:S(2)}) collective-permute-start(bf16[2,2,3,1,1,512]{5,4,2,1,3,0:T(2,128)(2,1)S(1)} %fusion.36), channel_id=1, source_target_pairs={{15,0},{0,1},{1,2},{2,3},{3,4},{4,5},{5,6},{6,7},{7,8},{8,9},{9,10... | collective-permute-start | bytes 36872 | tf_op jit(solution)/shard_map/ppermute | solution.py:38
  9.4 17.6 %collective-permute-start.2 = (bf16[2,2,3,1,4,512]{5,4,2,1,3,0:T(4,128)(2,1)S(1)}, bf16[2,2,3,1,4,512]{5,4,2,1,3,0:T(4,128)(2,1)S(1)}, u32[]{:S(2)}, u32[]{:S(2)}) collective-permute-start(bf16[2,2,3,1,4,512]{5,4,2,1,3,0:T(4,128)(2,1)S(1)} %pad_maximum_fusion.6), channel_id=1, source_target_pairs={{16,0},{32,16},{48,32},{64,48},{80,64},{96,80},{112,96},{128,112},... | collective-permute-start | bytes 147464 | tf_op jit(solution)/shard_map/ppermute | solution.py:38
  25.5 4.7 %collective-permute-start.3 = (bf16[2,2,3,1,4,512]{5,4,2,1,3,0:T(4,128)(2,1)S(1)}, bf16[2,2,3,1,4,512]{5,4,2,1,3,0:T(4,128)(2,1)S(1)}, u32[]{:S(2)}, u32[]{:S(2)}) collective-permute-start(bf16[2,2,3,1,4,512]{5,4,2,1,3,0:T(4,128)(2,1)S(1)} %pad_maximum_fusion.7), channel_id=1, source_target_pairs={{1008,0},{0,16},{16,32},{32,48},{48,64},{64,80},{80,96},{96,112},{... | collective-permute-start | bytes 147464 | tf_op jit(solution)/shard_map/ppermute | solution.py:38
  27.0 3.3 %copy-start.5 = (bf16[2,2,3,1,4,512]{5,4,2,1,3,0:T(4,128)(2,1)}, bf16[2,2,3,1,4,512]{5,4,2,1,3,0:T(4,128)(2,1)S(1)}, u32[]{:S(2)}) copy-start(bf16[2,2,3,1,4,512]{5,4,2,1,3,0:T(4,128)(2,1)S(1)} %collective-permute-done.2) | copy-start | bytes 147460
  30.2 0.6 copy-start.7
  34.2 7.2 %copy-start.2 = (bf16[2,4,3,1,4,512]{5,4,3,2,1,0:T(4,128)(2,1)}, bf16[2,4,3,1,4,512]{5,4,3,2,1,0:T(4,128)(2,1)S(1)}, u32[]{:S(2)}) copy-start(bf16[2,4,3,1,4,512]{5,4,3,2,1,0:T(4,128)(2,1)S(1)} %get-tuple-element.6) | copy-start | bytes 294916
  34.8 16.7 %copy-start.1 = (bf16[24,2,4,3,1,4,512]{6,5,4,3,2,1,0:T(4,128)(2,1)S(1)}, bf16[24,2,4,3,1,4,512]{6,5,4,3,2,1,0:T(4,128)(2,1)}, u32[]{:S(2)}) copy-start(bf16[24,2,4,3,1,4,512]{6,5,4,3,2,1,0:T(4,128)(2,1)} %param.10) | copy-start | bytes 7077892
  34.9 11.9 %collective-permute-start.4 = (bf16[2,2,3,1,1,512]{5,4,2,1,3,0:T(2,128)(2,1)S(1)}, bf16[2,2,3,1,1,512]{5,4,2,1,3,0:T(2,128)(2,1)S(1)}, u32[]{:S(2)}, u32[]{:S(2)}) collective-permute-start(bf16[2,2,3,1,1,512]{5,4,2,1,3,0:T(2,128)(2,1)S(1)} %pad_maximum_fusion.11), channel_id=1, source_target_pairs={{1,0},{2,1},{3,2},{4,3},{5,4},{6,5},{7,6},{8,7},{9,8},{10,9},{11,1... | collective-permute-start | bytes 36872 | tf_op jit(solution)/shard_map/ppermute | solution.py:38
  38.6 7.5 %collective-permute-start.5 = (bf16[2,2,3,1,1,512]{5,4,2,1,3,0:T(2,128)(2,1)S(1)}, bf16[2,2,3,1,1,512]{5,4,2,1,3,0:T(2,128)(2,1)S(1)}, u32[]{:S(2)}, u32[]{:S(2)}) collective-permute-start(bf16[2,2,3,1,1,512]{5,4,2,1,3,0:T(2,128)(2,1)S(1)} %fusion.35), channel_id=1, source_target_pairs={{15,0},{0,1},{1,2},{2,3},{3,4},{4,5},{5,6},{6,7},{7,8},{8,9},{9,10... | collective-permute-start | bytes 36872 | tf_op jit(solution)/shard_map/ppermute | solution.py:38
  41.2 6.3 %collective-permute-start.6 = (bf16[2,2,3,1,4,512]{5,4,2,1,3,0:T(4,128)(2,1)S(1)}, bf16[2,2,3,1,4,512]{5,4,2,1,3,0:T(4,128)(2,1)S(1)}, u32[]{:S(2)}, u32[]{:S(2)}) collective-permute-start(bf16[2,2,3,1,4,512]{5,4,2,1,3,0:T(4,128)(2,1)S(1)} %pad_maximum_fusion.9), channel_id=1, source_target_pairs={{16,0},{32,16},{48,32},{64,48},{80,64},{96,80},{112,96},{128,112},... | collective-permute-start | bytes 147464 | tf_op jit(solution)/shard_map/ppermute | solution.py:38
  41.5 6.0 %collective-permute-start.7 = (bf16[2,2,3,1,4,512]{5,4,2,1,3,0:T(4,128)(2,1)S(1)}, bf16[2,2,3,1,4,512]{5,4,2,1,3,0:T(4,128)(2,1)S(1)}, u32[]{:S(2)}, u32[]{:S(2)}) collective-permute-start(bf16[2,2,3,1,4,512]{5,4,2,1,3,0:T(4,128)(2,1)S(1)} %pad_maximum_fusion.10), channel_id=1, source_target_pairs={{1008,0},{0,16},{16,32},{32,48},{48,64},{64,80},{80,96},{96,112},{... | collective-permute-start | bytes 147464 | tf_op jit(solution)/shard_map/ppermute | solution.py:38
  47.5 0.6 copy-start.6
  47.5 0.6 copy-start.8
  48.2 4.6 %copy-start.9 = (s32[1,4,512]{2,1,0:T(4,128)S(1)}, s32[1,4,512]{2,1,0:T(4,128)}, u32[]{:S(2)}) copy-start(s32[1,4,512]{2,1,0:T(4,128)} %param.9) | copy-start | bytes 24580

commit v5 on v4

--- a/solution.py
+++ b/solution.py
@@ -1,3 +1,5 @@
+import functools
+
 import jax
 import jax.numpy as jnp
 from jax import lax
@@ -198,7 +200,7 @@
     ]
 
 
-def hop_kernel(v_ref, u_ref, az_ref, bz_ref, at_ref, bt_ref, out_ref):
+def sweep_kernel(last, v_ref, u_ref, az_ref, bz_ref, at_ref, bt_ref, src_ref, clov_ref, it_ref, *out_refs):
     width = v_ref.shape[-1]
     wide = nested_read(v_ref, 4)
     column = lax.broadcasted_iota(jnp.int32, wide[0][0][0].shape, 1) % LX
@@ -241,18 +243,49 @@
             behind = nested_read(bz_ref if mu == 2 else bt_ref, 2)
         accumulate(nested_expand(nested_mix(links, ahead, False), mu, -1.0))
         accumulate(nested_expand(behind, mu, 1.0))
+    half = [[[None] * 3 for _ in range(4)] for _ in range(2)]
     for part in range(2):
         for spin in range(4):
             for color in range(3):
-                out_ref[(part * 4 + spin) * 3 + color] = total[part][spin][color]
-
-
-def hopping(spinor, gauge_links):
+                index = (part * 4 + spin) * 3 + color
+                diagonal = 4.0 + mass_shift + clov_ref[spin * 3 + color]
+                iterate = it_ref[index]
+                resid = src_ref[index].astype(jnp.float32) - diagonal * iterate + 0.5 * total[part][spin][color]
+                if last:
+                    out_refs[0][index] = resid.astype(jnp.bfloat16)
+                else:
+                    new = iterate + resid / diagonal
+                    out_refs[0][index] = new
+                    rounded = new.astype(jnp.bfloat16)
+                    out_refs[1][index] = rounded
+                    half[part][spin][color] = rounded.astype(jnp.float32)
+    if last:
+        return
+    sends = (
+        nested_project(half, 2, -1.0),
+        nested_project(half, 3, -1.0),
+        nested_project(nested_mix(link(2), half, True), 2, 1.0),
+        nested_project(nested_mix(link(3), half, True), 3, 1.0),
+    )
+    for ref, send in zip(out_refs[2:], sends):
+        for part in range(2):
+            for slot in range(2):
+                for color in range(3):
+                    ref[(part * 2 + slot) * 3 + color] = send[part][slot][color].astype(jnp.bfloat16)
+
+
+def first_sends(spinor, gauge_links):
     wide = spinor.astype(jnp.float32)
-    fwd_z = project(wide, 2, -1.0).astype(jnp.bfloat16)
-    fwd_t = project(wide, 3, -1.0).astype(jnp.bfloat16)
-    back_z = project(color_mix(gauge_links[2], spinor, True), 2, 1.0).astype(jnp.bfloat16)
-    back_t = project(color_mix(gauge_links[3], spinor, True), 3, 1.0).astype(jnp.bfloat16)
+    return (
+        project(wide, 2, -1.0).astype(jnp.bfloat16),
+        project(wide, 3, -1.0).astype(jnp.bfloat16),
+        project(color_mix(gauge_links[2], spinor, True), 2, 1.0).astype(jnp.bfloat16),
+        project(color_mix(gauge_links[3], spinor, True), 3, 1.0).astype(jnp.bfloat16),
+    )
+
+
+def sweep(last, spinor, gauge_links, sends, source, clover_diag, iterate):
+    fwd_z, fwd_t, back_z, back_t = sends
     halves = [
         halo(fwd_z, GZ, 4, 1),
         halo(back_z, GZ, 4, -1),
@@ -264,16 +297,36 @@
     width = shape[5]
     flat = [half.reshape(12, rows, width) for half in halves]
     links = gauge_links.reshape(4, 18, rows, width)
-    total = pl.pallas_call(
-        hop_kernel,
-        out_shape=jax.ShapeDtypeStruct((24, rows, width), jnp.float32),
-        in_specs=[pl.BlockSpec(memory_space=pltpu.VMEM)] * 6,
-        out_specs=pl.BlockSpec(memory_space=pltpu.VMEM),
+    full = jax.ShapeDtypeStruct((24, rows, width), jnp.float32)
+    if last:
+        out_shape = [full.update(dtype=jnp.bfloat16)]
+    else:
+        part = jax.ShapeDtypeStruct((12, rows, width), jnp.bfloat16)
+        out_shape = [full, full.update(dtype=jnp.bfloat16), part, part, part, part]
+    outs = pl.pallas_call(
+        functools.partial(sweep_kernel, last),
+        out_shape=out_shape,
+        in_specs=[pl.BlockSpec(memory_space=pltpu.VMEM)] * 9,
+        out_specs=[pl.BlockSpec(memory_space=pltpu.VMEM)] * len(out_shape),
         cost_estimate=pl.CostEstimate(
-            flops=24 * 1024 * rows * width // 8, bytes_accessed=2 * 160 * rows * width, transcendentals=0
+            flops=24 * 1200 * rows * width // 8, bytes_accessed=2 * 200 * rows * width, transcendentals=0
         ),
-    )(spinor.reshape(24, rows, width), links, *flat)
-    return total.reshape(shape)
+    )(
+        spinor.reshape(24, rows, width),
+        links,
+        *flat,
+        source.reshape(24, rows, width),
+        clover_diag.reshape(12, rows, width),
+        iterate.reshape(24, rows, width),
+    )
+    if last:
+        return outs[0].reshape(shape)
+    half_shape = (2, 2, 3) + shape[3:]
+    return (
+        outs[0].reshape(shape),
+        outs[1].reshape(shape),
+        tuple(out.reshape(half_shape) for out in outs[2:]),
+    )
 
 
 def shards(source, gauge_links, clover_diag, agg_map, prolong, coarse_inverse):
@@ -282,11 +335,11 @@
     source_wide = source.astype(jnp.float32)
     first_iter = source_wide / diagonal
     first_half = first_iter.astype(jnp.bfloat16)
-    first_resid = source_wide - diagonal * first_iter + 0.5 * hopping(first_half, gauge_links)
-    second_iter = first_iter + first_resid / diagonal
-    second_half = second_iter.astype(jnp.bfloat16)
-    second_resid = source_wide - diagonal * second_iter + 0.5 * hopping(second_half, gauge_links)
-    resid_half = second_resid.astype(jnp.bfloat16)
+    sends = first_sends(first_half, gauge_links)
+    second_iter, second_half, sends = sweep(
+        False, first_half, gauge_links, sends, source, clover_diag, first_iter
+    )
+    resid_half = sweep(True, second_half, gauge_links, sends, source, clover_diag, second_iter)
     projected = jnp.einsum(
         "vrsctzn,rsctzn->vtzn", prolong, resid_half, preferred_element_type=jnp.float32
     )

time: 100 us -> 103 us (1.030)
  local copies, waits for them, and re-layouts: 1.79 us -> 4.28 us
  waiting for transfers between devices: 7.47 us -> 5.61 us
  starting transfers between devices: 28 us -> 29.4 us
    slice x0 -> x3, local copies, waits for them, and re-layouts: none -> 2.49 us  [the longest x1 0.84 us: halo(): edge = lax.slice_in_dim(block, size - 1, size, axis=dim)]
    mul x2 -> x0, other arithmetic: 1.94 us -> none  [the longest x1 0.97 us: shards(): 0.5 * hopping(first_half, gauge_links)]
    ppermute x8, waiting for transfers between devices: 7.47 us -> 5.61 us  [shifted(): return lax.ppermute(block, axis, route)]
    ppermute x8, starting transfers between devices: 28 us -> 29.4 us  [shifted(): return lax.ppermute(block, axis, route)]
  transfers between devices with their start and end apart: 8 -> 8, of which waited for: 2 -> 4; matrix products, arithmetic and copies ran while one was open for 5% -> 7% of each run, Pallas kernels for 0% -> 0%
where the time goes in v5:
time: 103 us; the launch traced here: 102 us
  blocking collectives  44 us (43%)
  starting transfers between devices  29.4 us (29%)
  other arithmetic  12.2 us (12%)
  waiting for transfers between devices  5.61 us (5%)
  Pallas kernels  5.27 us (5%)
  local copies, waits for them, and re-layouts  4.28 us (4%)
    ppermute x8, starting transfers between devices, shifted(): return lax.ppermute(block, axis, route)  29.4 us
    psum x2, blocking collectives, shards(): coarse_resid = lax.psum(lax.psum(partial_sum.reshape(-1), 'gx'), 'gy')  25 us
    psum x1, blocking collectives, shards(): lax.psum(lax.psum(padded, 'gx'), 'gy').reshape(NAGG, vectors)  11.1 us
    psum x1, blocking collectives, shards(): lax.psum(padded, 'gx')  7.89 us
    ppermute x8, waiting for transfers between devices, shifted(): return lax.ppermute(block, axis, route)  5.61 us
    pallas_call x2, Pallas kernels, sweep(): pl.pallas_call(functools.partial(sweep_kernel, last), out_shape=out_shape...  5.27 us
    unnamed x3, other arithmetic  2.22 us
    concatenate x2, other arithmetic, halo(): return jnp.concatenate([shifted(edge, axis, 1), inner], axis=dim)  2.15 us
  transfers between devices with their start and end apart: 8, of which 4 were waited for; matrix products, arithmetic and copies ran while one was open for 7% of the time, Pallas kernels for 0%

profile of v5, /device:TPU:10, one launch (start us, length us, event | category | flops | bytes accessed | tf_op | source)
XLA Modules:
  0.0 102.1 jit_solution(446913896726763084)
XLA Ops:
  0.0 0.0 copy-start
  0.0 1.0 add_bitcast_fusion
  1.0 1.7 %bitcast_convert_fusion.1 = (f32[2,4,3,1,4,512]{5,4,2,3,1,0:T(4,128)S(1)}, bf16[2,4,3,1,4,512]{5,4,3,2,1,0:T(4,128)(2,1)S(1)}, f32[2,4,3,1,4,512]{5,4,3,2,1,0:T(4,128)}) fusion(f32[4,3,4,512]{3,2,1,0:T(4,128)S(1)} %add_bitcast_fusion, bf16[2,4,3,1,4,512]{5,4,3,2,1,0:T(4,128)(2,1)} %param.6), kind=kLoop, calls=%fused_computation.31 | loop fusion | flops 196608 | bytes 688128 | tf_op jit(solution)/shard_map/convert_element_type | solution.py:278
  2.8 2.4 %collective-permute-start = (bf16[2,2,3,1,1,512]{5,4,2,1,3,0:T(2,128)(2,1)S(1)}, bf16[2,2,3,1,1,512]{5,4,2,1,3,0:T(2,128)(2,1)S(1)}, u32[]{:S(2)}, u32[]{:S(2)}) collective-permute-start(bf16[2,2,3,1,1,512]{5,4,2,1,3,0:T(2,128)(2,1)S(1)} %pad_maximum_fusion.8), channel_id=1, source_target_pairs={{1,0},{2,1},{3,2},{4,3},{5,4},{6,5},{7,6},{8,7},{9,8},{10,9},{11,1... | collective-permute-start | bytes 36872 | tf_op jit(solution)/shard_map/ppermute | solution.py:40
  5.3 15.9 %collective-permute-start.2 = (bf16[2,2,3,1,4,512]{5,4,2,1,3,0:T(4,128)(2,1)S(1)}, bf16[2,2,3,1,4,512]{5,4,2,1,3,0:T(4,128)(2,1)S(1)}, u32[]{:S(2)}, u32[]{:S(2)}) collective-permute-start(bf16[2,2,3,1,4,512]{5,4,2,1,3,0:T(4,128)(2,1)S(1)} %pad_maximum_fusion.4), channel_id=1, source_target_pairs={{16,0},{32,16},{48,32},{64,48},{80,64},{96,80},{112,96},{128,112},... | collective-permute-start | bytes 147464 | tf_op jit(solution)/shard_map/ppermute | solution.py:40
  21.3 0.8 bitcast_convert_fusion.3
  22.2 0.1 add_add_fusion.5
  22.2 0.1 add_add_fusion.4
  22.3 0.1 add_add_fusion.3
  22.6 0.1 fusion.23
  22.6 3.4 %collective-permute-start.1 = (bf16[2,2,3,1,1,512]{5,4,2,1,3,0:T(2,128)(2,1)S(1)}, bf16[2,2,3,1,1,512]{5,4,2,1,3,0:T(2,128)(2,1)S(1)}, u32[]{:S(2)}, u32[]{:S(2)}) collective-permute-start(bf16[2,2,3,1,1,512]{5,4,2,1,3,0:T(2,128)(2,1)S(1)} %fusion.23), channel_id=1, source_target_pairs={{15,0},{0,1},{1,2},{2,3},{3,4},{4,5},{5,6},{6,7},{7,8},{8,9},{9,10... | collective-permute-start | bytes 36872 | tf_op jit(solution)/shard_map/ppermute | solution.py:40
  26.1 0.1 subtract_add_fusion.2
  26.1 0.0 copy-start.1
  26.1 0.1 subtract_add_fusion.1
  26.2 0.1 subtract_add_fusion
  26.3 0.0 copy-done.2
  26.5 0.0 collective-permute-start.3
  26.5 0.1 slice_maximum_fusion
  26.6 2.4 %collective-permute-done.1 = bf16[2,2,3,1,1,512]{5,4,2,1,3,0:T(2,128)(2,1)S(1)} collective-permute-done((bf16[2,2,3,1,1,512]{5,4,2,1,3,0:T(2,128)(2,1)S(1)}, bf16[2,2,3,1,1,512]{5,4,2,1,3,0:T(2,128)(2,1)S(1)}, u32[]{:S(2)}, u32[]{:S(2)}) %collective-permute-start.1) | collective-permute-done | bytes 12320 | tf_op jit(solution)/shard_map/ppermute | solution.py:40
  29.0 0.7 fusion.16
  29.6 0.0 collective-permute-done
  29.6 0.7 pad_maximum_fusion.3
  30.3 0.0 collective-permute-done.2
  30.3 0.9 collective-permute-done.3
  31.2 0.0 copy-done.6
  31.2 0.6 copy-done.7
  31.9 2.8 %shard_map.64 = (f32[24,4,512]{2,1,0:T(4,128)}, bf16[24,4,512]{2,1,0:T(4,128)(2,1)}, bf16[12,4,512]{2,1,0:T(4,128)(2,1)}, bf16[12,4,512]{2,1,0:T(4,128)(2,1)}, b...) custom-call(bf16[24,4,512]{2,1,0:T(4,128)(2,1)} %bitcast.347, bf16[4,18,4,512]{3,2,1,0:T(4,128)(2,1)} %bitcast.340, ...), custom_call_target="tpu_custom_call" | custom-call | flops 7372800 | bytes 819200 | tf_op jit(solution)/shard_map/pallas_call | solution.py:306
  34.6 0.8 slice.480
  35.5 3.4 %collective-permute-start.5 = (bf16[2,2,3,1,1,512]{5,4,2,1,0,3:T(2,128)(2,1)S(1)}, bf16[2,2,3,1,1,512]{5,4,2,1,0,3:T(2,128)(2,1)S(1)}, u32[]{:S(2)}, u32[]{:S(2)}) collective-permute-start(bf16[2,2,3,1,1,512]{5,4,2,1,0,3:T(2,128)(2,1)S(1)} %slice.480), channel_id=1, source_target_pairs={{15,0},{0,1},{1,2},{2,3},{3,4},{4,5},{5,6},{6,7},{7,8},{8,9},{9,10... | collective-permute-start | bytes 36872 | tf_op jit(solution)/shard_map/ppermute | solution.py:40
  38.9 0.8 slice.479
  39.7 0.8 slice.478
  40.5 3.7 %collective-permute-start.4 = (bf16[2,2,3,1,1,512]{5,4,2,1,0,3:T(2,128)(2,1)S(1)}, bf16[2,2,3,1,1,512]{5,4,2,1,0,3:T(2,128)(2,1)S(1)}, u32[]{:S(2)}, u32[]{:S(2)}) collective-permute-start(bf16[2,2,3,1,1,512]{5,4,2,1,0,3:T(2,128)(2,1)S(1)} %slice.479), channel_id=1, source_target_pairs={{1,0},{2,1},{3,2},{4,3},{5,4},{6,5},{7,6},{8,7},{9,8},{10,9},{11,1... | collective-permute-start | bytes 36872 | tf_op jit(solution)/shard_map/ppermute | solution.py:40
  44.2 0.0 collective-permute-start.6
  44.2 0.5 collective-permute-start.7
  44.7 0.0 collective-permute-done.5
  44.7 1.5 %pad_maximum_fusion.7 = bf16[2,2,3,1,4,512]{5,4,2,1,0,3:T(4,128)(2,1)} fusion(bf16[2,2,3,1,3,512]{5,4,2,1,0,3:T(4,128)(2,1)} %bitcast.358, bf16[2,2,3,1,1,512]{5,4,2,1,0,3:T(2,128)(2,1)S(1)} %collective-permute-done.5), kind=kLoop, calls=%fused_computation.46 | loop fusion | flops 98304 | bytes 98304 | tf_op jit(solution)/shard_map/concatenate | solution.py:123
  46.2 1.3 %collective-permute-done.4 = bf16[2,2,3,1,1,512]{5,4,2,1,0,3:T(2,128)(2,1)S(1)} collective-permute-done((bf16[2,2,3,1,1,512]{5,4,2,1,0,3:T(2,128)(2,1)S(1)}, bf16[2,2,3,1,1,512]{5,4,2,1,0,3:T(2,128)(2,1)S(1)}, u32[]{:S(2)}, u32[]{:S(2)}) %collective-permute-start.4) | collective-permute-done | bytes 12320 | tf_op jit(solution)/shard_map/ppermute | solution.py:40
  47.5 0.7 pad_maximum_fusion.6
  48.2 0.0 collective-permute-done.6
  48.2 1.0 collective-permute-done.7
  49.2 0.0 copy-done.4
  49.2 0.6 copy-done.5
  49.8 2.5 %shard_map.65 = bf16[24,4,512]{2,1,0:T(4,128)(2,1)} custom-call(bf16[24,4,512]{2,1,0:T(4,128)(2,1)} %get-tuple-element.12.v_ref, bf16[4,18,4,512]{3,2,1,0:T(4,128)(2,1)} %bitcast.341, bf16[12,4,512]{2,1,0:T(4,128)(2,1)} %bitcast.352, bf16[12,4,512]{2,1,0:T(4,128)(2,1)} %bitcast.351, bf16[12,4,512]{2,1,0:T(4,128)(2,1)} %bitcast.359, ...), custom_call_target="tpu_custom_call" | custom-call | flops 7372800 | bytes 819200 | tf_op jit(solution)/shard_map/pallas_call | solution.py:306
  52.3 0.9 convert.94
  53.2 0.0 copy-done.1
  53.2 1.3 %multiply_reduce_fusion.1 = f32[4,512,24]{1,0,2:T(4,128)S(1)} fusion(f32[4,512,3,2,4]{1,0,2,4,3:T(4,128)S(1)} %convert.94, bf16[24,2,4,3,1,4,512]{6,5,4,3,2,1,0:T(4,128)(2,1)S(1)} %copy-done.1), kind=kLoop, calls=%fused_computation.1 | loop fusion | flops 3489792 | bytes 2752512
  54.5 0.0 copy-start.3
  54.5 0.0 copy-done.8
  54.5 0.2 convolution_bitcast_fusion
  54.7 0.2 convolution_bitcast_fusion.1
  54.9 0.2 fusion.1
  55.1 0.1 copy.44
  55.2 0.1 reshape.1288
  55.3 11.9 %psum.28 = f32[768]{0:T(1024)S(1)} all-reduce(f32[768]{0:T(1024)S(1)} %reshape.1288), channel_id=1, replica_groups=mesh['ta'=64,'gy'=4,'gx'=4] {'gx'}, use_global_device_ids=true, to_apply=%region_0.0 | all-reduce | flops 768 | bytes 6144 | tf_op jit(solution)/shard_map/psum | solution.py:357
  67.2 13.2 %psum.29 = f32[768]{0:T(1024)S(1)} all-reduce(f32[768]{0:T(1024)S(1)} %psum.28), channel_id=1, replica_groups=mesh['ta'=64,'gy'=4,'gx'=4] {'gy'}, use_global_device_ids=true, to_apply=%region_1.0 | all-reduce | flops 768 | bytes 6144 | tf_op jit(solution)/shard_map/psum | solution.py:357
  80.3 0.2 fusion.2
  80.5 0.3 dynamic_update_slice.3
  80.8 7.9 %psum.30 = bf16[768]{0:T(1024)(128)(2,1)S(1)} all-reduce(bf16[768]{0:T(1024)(128)(2,1)S(1)} %dynamic_update_slice.3), channel_id=1, replica_groups=mesh['ta'=64,'gy'=4,'gx'=4] {'gx'}, use_global_device_ids=true, to_apply=%region_2.0 | all-reduce | flops 768 | bytes 3072 | tf_op jit(solution)/shard_map/psum | solution.py:364
  88.7 0.1 reshape.1289
  88.8 11.1 %psum.31 = bf16[32,24]{1,0:T(8,128)(2,1)S(1)} all-reduce(bf16[32,24]{1,0:T(8,128)(2,1)S(1)} %reshape.1289), channel_id=1, replica_groups=mesh['ta'=64,'gy'=4,'gx'=4] {'gy'}, use_global_device_ids=true, to_apply=%region_3.0 | all-reduce | flops 768 | bytes 3072 | tf_op jit(solution)/shard_map/psum | solution.py:364
  99.8 0.2 convolution_convert_fusion
  100.0 0.1 fusion.15
  100.1 1.3 %multiply_reduce_fusion = f32[4,512,2,4,3]{1,0,4,3,2:T(4,128)S(1)} fusion(f32[4,512,24]{1,0,2:T(4,128)S(1)} %fusion.15, bf16[24,2,4,3,1,4,512]{6,5,4,3,2,1,0:T(4,128)(2,1)S(1)} %copy-done.1), kind=kLoop, calls=%fused_computation | loop fusion | flops 3489792 | bytes 2752512 | tf_op jit(solution)/shard_map/vrsctzn,vtzn->rsctzn/dot_general | solution.py:368
  101.4 0.7 bitcast_add_fusion
  (35 shorter events, 0.6 us)
Async XLA Ops:
  0.0 80.3 %copy-start = (f32[1,48,768]{2,1,0:T(8,128)S(1)}, f32[1,48,768]{2,1,0:T(8,128)}, u32[]{:S(2)}) copy-start(f32[1,48,768]{2,1,0:T(8,128)} %param.11) | copy-start | bytes 442372
  2.6 23.6 %copy-start.2 = (bf16[2,4,3,1,4,512]{5,4,3,2,1,0:T(4,128)(2,1)}, bf16[2,4,3,1,4,512]{5,4,3,2,1,0:T(4,128)(2,1)S(1)}, u32[]{:S(2)}) copy-start(bf16[2,4,3,1,4,512]{5,4,3,2,1,0:T(4,128)(2,1)S(1)} %get-tuple-element.18) | copy-start | bytes 294916
  2.8 26.9 %collective-permute-start = (bf16[2,2,3,1,1,512]{5,4,2,1,3,0:T(2,128)(2,1)S(1)}, bf16[2,2,3,1,1,512]{5,4,2,1,3,0:T(2,128)(2,1)S(1)}, u32[]{:S(2)}, u32[]{:S(2)}) collective-permute-start(bf16[2,2,3,1,1,512]{5,4,2,1,3,0:T(2,128)(2,1)S(1)} %pad_maximum_fusion.8), channel_id=1, source_target_pairs={{1,0},{2,1},{3,2},{4,3},{5,4},{6,5},{7,6},{8,7},{9,8},{10,9},{11,1... | collective-permute-start | bytes 36872 | tf_op jit(solution)/shard_map/ppermute | solution.py:40
  5.3 25.0 %collective-permute-start.2 = (bf16[2,2,3,1,4,512]{5,4,2,1,3,0:T(4,128)(2,1)S(1)}, bf16[2,2,3,1,4,512]{5,4,2,1,3,0:T(4,128)(2,1)S(1)}, u32[]{:S(2)}, u32[]{:S(2)}) collective-permute-start(bf16[2,2,3,1,4,512]{5,4,2,1,3,0:T(4,128)(2,1)S(1)} %pad_maximum_fusion.4), channel_id=1, source_target_pairs={{16,0},{32,16},{48,32},{64,48},{80,64},{96,80},{112,96},{128,112},... | collective-permute-start | bytes 147464 | tf_op jit(solution)/shard_map/ppermute | solution.py:40
  22.6 6.4 %collective-permute-start.1 = (bf16[2,2,3,1,1,512]{5,4,2,1,3,0:T(2,128)(2,1)S(1)}, bf16[2,2,3,1,1,512]{5,4,2,1,3,0:T(2,128)(2,1)S(1)}, u32[]{:S(2)}, u32[]{:S(2)}) collective-permute-start(bf16[2,2,3,1,1,512]{5,4,2,1,3,0:T(2,128)(2,1)S(1)} %fusion.23), channel_id=1, source_target_pairs={{15,0},{0,1},{1,2},{2,3},{3,4},{4,5},{5,6},{6,7},{7,8},{8,9},{9,10... | collective-permute-start | bytes 36872 | tf_op jit(solution)/shard_map/ppermute | solution.py:40
  26.1 27.1 %copy-start.1 = (bf16[24,2,4,3,1,4,512]{6,5,4,3,2,1,0:T(4,128)(2,1)S(1)}, bf16[24,2,4,3,1,4,512]{6,5,4,3,2,1,0:T(4,128)(2,1)}, u32[]{:S(2)}) copy-start(bf16[24,2,4,3,1,4,512]{6,5,4,3,2,1,0:T(4,128)(2,1)} %param.10) | copy-start | bytes 7077892
  26.5 4.7 %collective-permute-start.3 = (bf16[2,2,3,1,4,512]{5,4,2,1,3,0:T(4,128)(2,1)S(1)}, bf16[2,2,3,1,4,512]{5,4,2,1,3,0:T(4,128)(2,1)S(1)}, u32[]{:S(2)}, u32[]{:S(2)}) collective-permute-start(bf16[2,2,3,1,4,512]{5,4,2,1,3,0:T(4,128)(2,1)S(1)} %pad_maximum_fusion.5), channel_id=1, source_target_pairs={{1008,0},{0,16},{16,32},{32,48},{48,64},{64,80},{80,96},{96,112},{... | collective-permute-start | bytes 147464 | tf_op jit(solution)/shard_map/ppermute | solution.py:40
  30.3 0.9 copy-start.6
  31.2 0.6 copy-start.7
  34.6 19.9 %copy-start.8 = (s32[1,4,512]{2,1,0:T(4,128)S(1)}, s32[1,4,512]{2,1,0:T(4,128)}, u32[]{:S(2)}) copy-start(s32[1,4,512]{2,1,0:T(4,128)} %param.9) | copy-start | bytes 24580
  35.5 9.3 %collective-permute-start.5 = (bf16[2,2,3,1,1,512]{5,4,2,1,0,3:T(2,128)(2,1)S(1)}, bf16[2,2,3,1,1,512]{5,4,2,1,0,3:T(2,128)(2,1)S(1)}, u32[]{:S(2)}, u32[]{:S(2)}) collective-permute-start(bf16[2,2,3,1,1,512]{5,4,2,1,0,3:T(2,128)(2,1)S(1)} %slice.480), channel_id=1, source_target_pairs={{15,0},{0,1},{1,2},{2,3},{3,4},{4,5},{5,6},{6,7},{7,8},{8,9},{9,10... | collective-permute-start | bytes 36872 | tf_op jit(solution)/shard_map/ppermute | solution.py:40
  40.5 7.0 %collective-permute-start.4 = (bf16[2,2,3,1,1,512]{5,4,2,1,0,3:T(2,128)(2,1)S(1)}, bf16[2,2,3,1,1,512]{5,4,2,1,0,3:T(2,128)(2,1)S(1)}, u32[]{:S(2)}, u32[]{:S(2)}) collective-permute-start(bf16[2,2,3,1,1,512]{5,4,2,1,0,3:T(2,128)(2,1)S(1)} %slice.479), channel_id=1, source_target_pairs={{1,0},{2,1},{3,2},{4,3},{5,4},{6,5},{7,6},{8,7},{9,8},{10,9},{11,1... | collective-permute-start | bytes 36872 | tf_op jit(solution)/shard_map/ppermute | solution.py:40
  44.2 4.0 %collective-permute-start.6 = (bf16[2,2,3,1,4,512]{5,4,2,1,0,3:T(4,128)(2,1)}, bf16[2,2,3,1,4,512]{5,4,2,1,0,3:T(4,128)(2,1)S(1)}, u32[]{:S(2)}, u32[]{:S(2)}) collective-permute-start(bf16[2,2,3,1,4,512]{5,4,2,1,0,3:T(4,128)(2,1)} %bitcast.368), channel_id=1, source_target_pairs={{16,0},{32,16},{48,32},{64,48},{80,64},{96,80},{112,96},{128,112},... | collective-permute-start | bytes 147464 | tf_op jit(solution)/shard_map/ppermute | solution.py:40
  44.2 4.9 %collective-permute-start.7 = (bf16[2,2,3,1,4,512]{5,4,2,1,0,3:T(4,128)(2,1)}, bf16[2,2,3,1,4,512]{5,4,2,1,0,3:T(4,128)(2,1)S(1)}, u32[]{:S(2)}, u32[]{:S(2)}) collective-permute-start(bf16[2,2,3,1,4,512]{5,4,2,1,0,3:T(4,128)(2,1)} %bitcast.367), channel_id=1, source_target_pairs={{1008,0},{0,16},{16,32},{32,48},{48,64},{64,80},{80,96},{96,112},{... | collective-permute-start | bytes 147464 | tf_op jit(solution)/shard_map/ppermute | solution.py:40
  48.2 1.0 copy-start.4
  49.2 0.6 copy-start.5
  54.5 46.9 %copy-start.3 = (f32[24,4,512]{2,1,0:T(4,128)S(1)}, f32[24,4,512]{2,1,0:T(4,128)}, u32[]{:S(2)}) copy-start(f32[24,4,512]{2,1,0:T(4,128)} %get-tuple-element.11.it_ref) | copy-start | bytes 589828

commit v6 on v5

--- a/solution.py
+++ b/solution.py
@@ -259,7 +259,7 @@
                     rounded = new.astype(jnp.bfloat16)
                     out_refs[1][index] = rounded
                     half[part][spin][color] = rounded.astype(jnp.float32)
-    if last:
+    if len(out_refs) < 3:
         return
     sends = (
         nested_project(half, 2, -1.0),
@@ -301,8 +301,7 @@
     if last:
         out_shape = [full.update(dtype=jnp.bfloat16)]
     else:
-        part = jax.ShapeDtypeStruct((12, rows, width), jnp.bfloat16)
-        out_shape = [full, full.update(dtype=jnp.bfloat16), part, part, part, part]
+        out_shape = [full, full.update(dtype=jnp.bfloat16)]
     outs = pl.pallas_call(
         functools.partial(sweep_kernel, last),
         out_shape=out_shape,
@@ -321,12 +320,8 @@
     )
     if last:
         return outs[0].reshape(shape)
-    half_shape = (2, 2, 3) + shape[3:]
-    return (
-        outs[0].reshape(shape),
-        outs[1].reshape(shape),
-        tuple(out.reshape(half_shape) for out in outs[2:]),
-    )
+    second_half = outs[1].reshape(shape)
+    return outs[0].reshape(shape), second_half, first_sends(second_half, gauge_links)
 
 
 def shards(source, gauge_links, clover_diag, agg_map, prolong, coarse_inverse):

time: 103 us -> 102 us (level)
  waiting for transfers between devices: 5.61 us -> 7.45 us
  local copies, waits for them, and re-layouts: 4.28 us -> 2.65 us
  starting transfers between devices: 29.4 us -> 28 us
  other arithmetic: 12.2 us -> 13.3 us
    ppermute x8, waiting for transfers between devices: 5.61 us -> 7.45 us  [shifted(): return lax.ppermute(block, axis, route)]
    slice x3 -> x1, local copies, waits for them, and re-layouts: 2.49 us -> 0.86 us  [color_mix(): spin_re = spinor[0].astype(jnp.float32)]
    ppermute x8, starting transfers between devices: 29.4 us -> 28 us  [shifted(): return lax.ppermute(block, axis, route)]
    convert_element_type x1 -> x2, other arithmetic: 1.65 us -> 2.56 us  [first_sends(): wide = spinor.astype(jnp.float32)]
  transfers between devices with their start and end apart: 8 -> 8, of which waited for: 4 -> 2; matrix products, arithmetic and copies ran while one was open for 7% -> 5% of each run, Pallas kernels for 0% -> 0%
where the time goes in v6:
time: 102 us; the launch traced here: 101 us
  blocking collectives  43.1 us (42%)
  starting transfers between devices  28 us (27%)
  other arithmetic  13.3 us (13%)
  waiting for transfers between devices  7.45 us (7%)
  Pallas kernels  5.11 us (5%)
  local copies, waits for them, and re-layouts  2.65 us (3%)
    ppermute x8, starting transfers between devices, shifted(): return lax.ppermute(block, axis, route)  28 us
    psum x2, blocking collectives, shards(): coarse_resid = lax.psum(lax.psum(partial_sum.reshape(-1), 'gx'), 'gy')  25 us
    psum x1, blocking collectives, shards(): lax.psum(lax.psum(padded, 'gx'), 'gy').reshape(NAGG, vectors)  10.4 us
    psum x1, blocking collectives, shards(): lax.psum(padded, 'gx')  7.72 us
    ppermute x8, waiting for transfers between devices, shifted(): return lax.ppermute(block, axis, route)  7.45 us
    pallas_call x2, Pallas kernels, sweep(): pl.pallas_call(functools.partial(sweep_kernel, last), out_shape=out_shape...  5.11 us
    convert_element_type x2, other arithmetic, first_sends(): wide = spinor.astype(jnp.float32)  2.56 us
    unnamed x3, other arithmetic  2.22 us
  transfers between devices with their start and end apart: 8, of which 2 were waited for; matrix products, arithmetic and copies ran while one was open for 5% of the time, Pallas kernels for 0%

profile of v6, /device:TPU:10, one launch (start us, length us, event | category | flops | bytes accessed | tf_op | source)
XLA Modules:
  0.0 101.3 jit_solution(4319553750918582338)
XLA Ops:
  0.0 1.0 add_bitcast_fusion
  1.0 1.7 %bitcast_convert_fusion.1 = (f32[2,4,3,1,4,512]{5,4,2,3,1,0:T(4,128)S(1)}, bf16[2,4,3,1,4,512]{5,4,3,2,1,0:T(4,128)(2,1)S(1)}, f32[2,4,3,1,4,512]{5,4,3,2,1,0:T(4,128)}) fusion(f32[4,3,4,512]{3,2,1,0:T(4,128)S(1)} %add_bitcast_fusion, bf16[2,4,3,1,4,512]{5,4,3,2,1,0:T(4,128)(2,1)} %param.6), kind=kLoop, calls=%fused_computation.35 | loop fusion | flops 196608 | bytes 688128 | tf_op jit(solution)/shard_map/convert_element_type | solution.py:278
  2.8 2.4 %collective-permute-start = (bf16[2,2,3,1,1,512]{5,4,2,1,3,0:T(2,128)(2,1)S(1)}, bf16[2,2,3,1,1,512]{5,4,2,1,3,0:T(2,128)(2,1)S(1)}, u32[]{:S(2)}, u32[]{:S(2)}) collective-permute-start(bf16[2,2,3,1,1,512]{5,4,2,1,3,0:T(2,128)(2,1)S(1)} %pad_maximum_fusion.12), channel_id=1, source_target_pairs={{1,0},{2,1},{3,2},{4,3},{5,4},{6,5},{7,6},{8,7},{9,8},{10,9},{11,1... | collective-permute-start | bytes 36872 | tf_op jit(solution)/shard_map/ppermute | solution.py:40
  5.2 0.8 bitcast_convert_fusion.3
  6.1 0.1 add_add_fusion.9
  6.2 0.1 add_add_fusion.10
  6.3 0.1 add_add_fusion.11
  6.5 0.1 fusion.27
  6.6 3.4 %collective-permute-start.1 = (bf16[2,2,3,1,1,512]{5,4,2,1,3,0:T(2,128)(2,1)S(1)}, bf16[2,2,3,1,1,512]{5,4,2,1,3,0:T(2,128)(2,1)S(1)}, u32[]{:S(2)}, u32[]{:S(2)}) collective-permute-start(bf16[2,2,3,1,1,512]{5,4,2,1,3,0:T(2,128)(2,1)S(1)} %fusion.27), channel_id=1, source_target_pairs={{15,0},{0,1},{1,2},{2,3},{3,4},{4,5},{5,6},{6,7},{7,8},{8,9},{9,10... | collective-permute-start | bytes 36872 | tf_op jit(solution)/shard_map/ppermute | solution.py:40
  10.1 15.7 %collective-permute-start.2 = (bf16[2,2,3,1,4,512]{5,4,2,1,3,0:T(4,128)(2,1)S(1)}, bf16[2,2,3,1,4,512]{5,4,2,1,3,0:T(4,128)(2,1)S(1)}, u32[]{:S(2)}, u32[]{:S(2)}) collective-permute-start(bf16[2,2,3,1,4,512]{5,4,2,1,3,0:T(4,128)(2,1)S(1)} %pad_maximum_fusion.6), channel_id=1, source_target_pairs={{16,0},{32,16},{48,32},{64,48},{80,64},{96,80},{112,96},{128,112},... | collective-permute-start | bytes 147464 | tf_op jit(solution)/shard_map/ppermute | solution.py:40
  25.7 0.1 subtract_add_fusion.6
  25.8 0.1 subtract_add_fusion.7
  25.9 0.1 subtract_add_fusion.8
  26.2 0.0 collective-permute-start.3
  26.2 0.1 slice_maximum_fusion.1
  26.3 0.0 collective-permute-done.1
  26.3 0.7 fusion.17
  27.0 0.7 pad_maximum_fusion.5
  27.6 0.0 collective-permute-done.2
  27.7 3.3 %collective-permute-done.3 = bf16[2,2,3,1,4,512]{5,4,2,1,3,0:T(4,128)(2,1)S(1)} collective-permute-done((bf16[2,2,3,1,4,512]{5,4,2,1,3,0:T(4,128)(2,1)S(1)}, bf16[2,2,3,1,4,512]{5,4,2,1,3,0:T(4,128)(2,1)S(1)}, u32[]{:S(2)}, u32[]{:S(2)}) %collective-permute-start.3) | collective-permute-done | bytes 49184 | tf_op jit(solution)/shard_map/ppermute | solution.py:40
  30.9 0.6 copy-done.7
  31.5 2.6 %shard_map.64 = (f32[24,4,512]{2,1,0:T(4,128)}, bf16[24,4,512]{2,1,0:T(4,128)(2,1)}) custom-call(bf16[24,4,512]{2,1,0:T(4,128)(2,1)} %bitcast.453, bf16[4,18,4,512]{3,2,1,0:T(4,128)(2,1)} %bitcast.445, bf16[12,4,512]{2,1,0:T(4,128)(2,1)} %bitcast.462, bf16[12,4,512]{2,1,0:T(4,128)(2,1)} %bitcast.461, bf16[12,4,512]{2,1,0:T(4,128)(2,1)} %bitcast.465, ...), custom_call_target="tpu_custom_call" | custom-call | flops 7372800 | bytes 819200 | tf_op jit(solution)/shard_map/pallas_call | solution.py:305
  34.1 0.9 convert.198
  35.2 0.1 slice_maximum_fusion
  35.2 0.9 fusion.94
  36.1 0.1 add_add_fusion.3
  36.2 0.1 add_add_fusion.4
  36.3 0.1 add_add_fusion.5
  36.3 0.0 copy-start.1
  36.4 0.1 subtract_add_fusion
  36.4 0.1 subtract_add_fusion.1
  36.5 0.1 subtract_add_fusion.2
  36.6 3.5 %collective-permute-start.4 = (bf16[2,2,3,1,1,512]{5,4,2,1,3,0:T(2,128)(2,1)S(1)}, bf16[2,2,3,1,1,512]{5,4,2,1,3,0:T(2,128)(2,1)S(1)}, u32[]{:S(2)}, u32[]{:S(2)}) collective-permute-start(bf16[2,2,3,1,1,512]{5,4,2,1,3,0:T(2,128)(2,1)S(1)} %pad_maximum_fusion.11), channel_id=1, source_target_pairs={{1,0},{2,1},{3,2},{4,3},{5,4},{6,5},{7,6},{8,7},{9,8},{10,9},{11,1... | collective-permute-start | bytes 36872 | tf_op jit(solution)/shard_map/ppermute | solution.py:40
  40.2 0.1 fusion.26
  40.3 2.5 %collective-permute-start.5 = (bf16[2,2,3,1,1,512]{5,4,2,1,3,0:T(2,128)(2,1)S(1)}, bf16[2,2,3,1,1,512]{5,4,2,1,3,0:T(2,128)(2,1)S(1)}, u32[]{:S(2)}, u32[]{:S(2)}) collective-permute-start(bf16[2,2,3,1,1,512]{5,4,2,1,3,0:T(2,128)(2,1)S(1)} %fusion.26), channel_id=1, source_target_pairs={{15,0},{0,1},{1,2},{2,3},{3,4},{4,5},{5,6},{6,7},{7,8},{8,9},{9,10... | collective-permute-start | bytes 36872 | tf_op jit(solution)/shard_map/ppermute | solution.py:40
  42.9 0.0 collective-permute-start.6
  43.0 0.0 copy-start.8
  43.1 0.5 collective-permute-start.7
  43.7 4.2 %collective-permute-done.5 = bf16[2,2,3,1,1,512]{5,4,2,1,3,0:T(2,128)(2,1)S(1)} collective-permute-done((bf16[2,2,3,1,1,512]{5,4,2,1,3,0:T(2,128)(2,1)S(1)}, bf16[2,2,3,1,1,512]{5,4,2,1,3,0:T(2,128)(2,1)S(1)}, u32[]{:S(2)}, u32[]{:S(2)}) %collective-permute-start.5) | collective-permute-done | bytes 12320 | tf_op jit(solution)/shard_map/ppermute | solution.py:40
  47.8 0.7 fusion.16
  48.5 0.0 collective-permute-done.4
  48.5 0.7 pad_maximum_fusion.8
  49.2 0.0 collective-permute-done.6
  49.2 0.6 copy-done.4
  49.8 0.0 copy-done.5
  49.8 2.5 %shard_map.65 = bf16[24,4,512]{2,1,0:T(4,128)(2,1)} custom-call(bf16[24,4,512]{2,1,0:T(4,128)(2,1)} %get-tuple-element.8.v_ref, bf16[4,18,4,512]{3,2,1,0:T(4,128)(2,1)} %bitcast.446, bf16[12,4,512]{2,1,0:T(4,128)(2,1)} %bitcast.458, bf16[12,4,512]{2,1,0:T(4,128)(2,1)} %bitcast.457, bf16[12,4,512]{2,1,0:T(4,128)(2,1)} %bitcast.463, ...), custom_call_target="tpu_custom_call" | custom-call | flops 7372800 | bytes 819200 | tf_op jit(solution)/shard_map/pallas_call | solution.py:305
  52.3 0.9 convert.185
  53.2 1.3 %multiply_reduce_fusion.1 = f32[4,512,24]{1,0,2:T(4,128)S(1)} fusion(f32[4,512,3,2,4]{1,0,2,4,3:T(4,128)S(1)} %convert.185, bf16[24,2,4,3,1,4,512]{6,5,4,3,2,1,0:T(4,128)(2,1)S(1)} %copy-done.1), kind=kLoop, calls=%fused_computation.1 | loop fusion | flops 3489792 | bytes 2752512
  54.5 0.2 convolution_bitcast_fusion
  54.7 0.2 convolution_bitcast_fusion.1
  54.9 0.2 fusion.1
  55.1 0.1 copy.74
  55.2 0.1 reshape.2141
  55.3 11.9 %psum.28 = f32[768]{0:T(1024)S(1)} all-reduce(f32[768]{0:T(1024)S(1)} %reshape.2141), channel_id=1, replica_groups=mesh['ta'=64,'gy'=4,'gx'=4] {'gx'}, use_global_device_ids=true, to_apply=%region_0.0 | all-reduce | flops 768 | bytes 6144 | tf_op jit(solution)/shard_map/psum | solution.py:352
  67.2 13.2 %psum.29 = f32[768]{0:T(1024)S(1)} all-reduce(f32[768]{0:T(1024)S(1)} %psum.28), channel_id=1, replica_groups=mesh['ta'=64,'gy'=4,'gx'=4] {'gy'}, use_global_device_ids=true, to_apply=%region_1.0 | all-reduce | flops 768 | bytes 6144 | tf_op jit(solution)/shard_map/psum | solution.py:352
  80.3 0.2 fusion.2
  80.5 0.3 dynamic_update_slice.3
  80.8 7.7 %psum.30 = bf16[768]{0:T(1024)(128)(2,1)S(1)} all-reduce(bf16[768]{0:T(1024)(128)(2,1)S(1)} %dynamic_update_slice.3), channel_id=1, replica_groups=mesh['ta'=64,'gy'=4,'gx'=4] {'gx'}, use_global_device_ids=true, to_apply=%region_2.0 | all-reduce | flops 768 | bytes 3072 | tf_op jit(solution)/shard_map/psum | solution.py:359
  88.5 0.1 reshape.2142
  88.6 10.4 %psum.31 = bf16[32,24]{1,0:T(8,128)(2,1)S(1)} all-reduce(bf16[32,24]{1,0:T(8,128)(2,1)S(1)} %reshape.2142), channel_id=1, replica_groups=mesh['ta'=64,'gy'=4,'gx'=4] {'gy'}, use_global_device_ids=true, to_apply=%region_3.0 | all-reduce | flops 768 | bytes 3072 | tf_op jit(solution)/shard_map/psum | solution.py:359
  99.0 0.2 convolution_convert_fusion
  99.2 0.1 fusion.15
  99.2 1.3 %multiply_reduce_fusion = f32[4,512,2,4,3]{1,0,4,3,2:T(4,128)S(1)} fusion(f32[4,512,24]{1,0,2:T(4,128)S(1)} %fusion.15, bf16[24,2,4,3,1,4,512]{6,5,4,3,2,1,0:T(4,128)(2,1)S(1)} %copy-done.1), kind=kLoop, calls=%fused_computation | loop fusion | flops 3489792 | bytes 2752512 | tf_op jit(solution)/shard_map/vrsctzn,vtzn->rsctzn/dot_general | solution.py:363
  100.6 0.7 bitcast_add_fusion
  (64 shorter events, 1.1 us)
Async XLA Ops:
  0.0 80.3 %copy-start = (f32[1,48,768]{2,1,0:T(8,128)S(1)}, f32[1,48,768]{2,1,0:T(8,128)}, u32[]{:S(2)}) copy-start(f32[1,48,768]{2,1,0:T(8,128)} %param.11) | copy-start | bytes 442372
  2.6 23.3 %copy-start.2 = (bf16[2,4,3,1,4,512]{5,4,3,2,1,0:T(4,128)(2,1)}, bf16[2,4,3,1,4,512]{5,4,3,2,1,0:T(4,128)(2,1)S(1)}, u32[]{:S(2)}) copy-start(bf16[2,4,3,1,4,512]{5,4,3,2,1,0:T(4,128)(2,1)S(1)} %get-tuple-element.10) | copy-start | bytes 294916
  2.8 24.2 %collective-permute-start = (bf16[2,2,3,1,1,512]{5,4,2,1,3,0:T(2,128)(2,1)S(1)}, bf16[2,2,3,1,1,512]{5,4,2,1,3,0:T(2,128)(2,1)S(1)}, u32[]{:S(2)}, u32[]{:S(2)}) collective-permute-start(bf16[2,2,3,1,1,512]{5,4,2,1,3,0:T(2,128)(2,1)S(1)} %pad_maximum_fusion.12), channel_id=1, source_target_pairs={{1,0},{2,1},{3,2},{4,3},{5,4},{6,5},{7,6},{8,7},{9,8},{10,9},{11,1... | collective-permute-start | bytes 36872 | tf_op jit(solution)/shard_map/ppermute | solution.py:40
  6.6 19.7 %collective-permute-start.1 = (bf16[2,2,3,1,1,512]{5,4,2,1,3,0:T(2,128)(2,1)S(1)}, bf16[2,2,3,1,1,512]{5,4,2,1,3,0:T(2,128)(2,1)S(1)}, u32[]{:S(2)}, u32[]{:S(2)}) collective-permute-start(bf16[2,2,3,1,1,512]{5,4,2,1,3,0:T(2,128)(2,1)S(1)} %fusion.27), channel_id=1, source_target_pairs={{15,0},{0,1},{1,2},{2,3},{3,4},{4,5},{5,6},{6,7},{7,8},{8,9},{9,10... | collective-permute-start | bytes 36872 | tf_op jit(solution)/shard_map/ppermute | solution.py:40
  10.1 17.6 %collective-permute-start.2 = (bf16[2,2,3,1,4,512]{5,4,2,1,3,0:T(4,128)(2,1)S(1)}, bf16[2,2,3,1,4,512]{5,4,2,1,3,0:T(4,128)(2,1)S(1)}, u32[]{:S(2)}, u32[]{:S(2)}) collective-permute-start(bf16[2,2,3,1,4,512]{5,4,2,1,3,0:T(4,128)(2,1)S(1)} %pad_maximum_fusion.6), channel_id=1, source_target_pairs={{16,0},{32,16},{48,32},{64,48},{80,64},{96,80},{112,96},{128,112},... | collective-permute-start | bytes 147464 | tf_op jit(solution)/shard_map/ppermute | solution.py:40
  26.2 4.7 %collective-permute-start.3 = (bf16[2,2,3,1,4,512]{5,4,2,1,3,0:T(4,128)(2,1)S(1)}, bf16[2,2,3,1,4,512]{5,4,2,1,3,0:T(4,128)(2,1)S(1)}, u32[]{:S(2)}, u32[]{:S(2)}) collective-permute-start(bf16[2,2,3,1,4,512]{5,4,2,1,3,0:T(4,128)(2,1)S(1)} %pad_maximum_fusion.7), channel_id=1, source_target_pairs={{1008,0},{0,16},{16,32},{32,48},{48,64},{64,80},{80,96},{96,112},{... | collective-permute-start | bytes 147464 | tf_op jit(solution)/shard_map/ppermute | solution.py:40
  27.6 3.3 %copy-start.6 = (bf16[2,2,3,1,4,512]{5,4,2,1,3,0:T(4,128)(2,1)}, bf16[2,2,3,1,4,512]{5,4,2,1,3,0:T(4,128)(2,1)S(1)}, u32[]{:S(2)}) copy-start(bf16[2,2,3,1,4,512]{5,4,2,1,3,0:T(4,128)(2,1)S(1)} %collective-permute-done.2) | copy-start | bytes 147460
  30.9 0.6 copy-start.7
  36.3 16.9 %copy-start.1 = (bf16[24,2,4,3,1,4,512]{6,5,4,3,2,1,0:T(4,128)(2,1)S(1)}, bf16[24,2,4,3,1,4,512]{6,5,4,3,2,1,0:T(4,128)(2,1)}, u32[]{:S(2)}) copy-start(bf16[24,2,4,3,1,4,512]{6,5,4,3,2,1,0:T(4,128)(2,1)} %param.10) | copy-start | bytes 7077892
  36.6 11.9 %collective-permute-start.4 = (bf16[2,2,3,1,1,512]{5,4,2,1,3,0:T(2,128)(2,1)S(1)}, bf16[2,2,3,1,1,512]{5,4,2,1,3,0:T(2,128)(2,1)S(1)}, u32[]{:S(2)}, u32[]{:S(2)}) collective-permute-start(bf16[2,2,3,1,1,512]{5,4,2,1,3,0:T(2,128)(2,1)S(1)} %pad_maximum_fusion.11), channel_id=1, source_target_pairs={{1,0},{2,1},{3,2},{4,3},{5,4},{6,5},{7,6},{8,7},{9,8},{10,9},{11,1... | collective-permute-start | bytes 36872 | tf_op jit(solution)/shard_map/ppermute | solution.py:40
  40.3 7.5 %collective-permute-start.5 = (bf16[2,2,3,1,1,512]{5,4,2,1,3,0:T(2,128)(2,1)S(1)}, bf16[2,2,3,1,1,512]{5,4,2,1,3,0:T(2,128)(2,1)S(1)}, u32[]{:S(2)}, u32[]{:S(2)}) collective-permute-start(bf16[2,2,3,1,1,512]{5,4,2,1,3,0:T(2,128)(2,1)S(1)} %fusion.26), channel_id=1, source_target_pairs={{15,0},{0,1},{1,2},{2,3},{3,4},{4,5},{5,6},{6,7},{7,8},{8,9},{9,10... | collective-permute-start | bytes 36872 | tf_op jit(solution)/shard_map/ppermute | solution.py:40
  42.9 6.3 %collective-permute-start.6 = (bf16[2,2,3,1,4,512]{5,4,2,1,3,0:T(4,128)(2,1)S(1)}, bf16[2,2,3,1,4,512]{5,4,2,1,3,0:T(4,128)(2,1)S(1)}, u32[]{:S(2)}, u32[]{:S(2)}) collective-permute-start(bf16[2,2,3,1,4,512]{5,4,2,1,3,0:T(4,128)(2,1)S(1)} %pad_maximum_fusion.9), channel_id=1, source_target_pairs={{16,0},{32,16},{48,32},{64,48},{80,64},{96,80},{112,96},{128,112},... | collective-permute-start | bytes 147464 | tf_op jit(solution)/shard_map/ppermute | solution.py:40
  43.0 11.5 %copy-start.8 = (s32[1,4,512]{2,1,0:T(4,128)S(1)}, s32[1,4,512]{2,1,0:T(4,128)}, u32[]{:S(2)}) copy-start(s32[1,4,512]{2,1,0:T(4,128)} %param.9) | copy-start | bytes 24580
  43.1 6.0 %collective-permute-start.7 = (bf16[2,2,3,1,4,512]{5,4,2,1,3,0:T(4,128)(2,1)S(1)}, bf16[2,2,3,1,4,512]{5,4,2,1,3,0:T(4,128)(2,1)S(1)}, u32[]{:S(2)}, u32[]{:S(2)}) collective-permute-start(bf16[2,2,3,1,4,512]{5,4,2,1,3,0:T(4,128)(2,1)S(1)} %pad_maximum_fusion.10), channel_id=1, source_target_pairs={{1008,0},{0,16},{16,32},{32,48},{48,64},{64,80},{80,96},{96,112},{... | collective-permute-start | bytes 147464 | tf_op jit(solution)/shard_map/ppermute | solution.py:40
  49.2 0.6 copy-start.4
  49.2 0.6 copy-start.5
  54.5 46.1 %copy-start.3 = (f32[24,4,512]{2,1,0:T(4,128)S(1)}, f32[24,4,512]{2,1,0:T(4,128)}, u32[]{:S(2)}) copy-start(f32[24,4,512]{2,1,0:T(4,128)} %get-tuple-element.7.it_ref) | copy-start | bytes 589828
